TPU v7x, 256 devices: a whole 4x4x8 slice. The times are simulated.
256 devices in a mesh: gx: 16 (over y, z_lo), gy: 16 (over x, z_hi, core).
Axes of the slice: x: 4, y: 4, z: 8 (z_hi: 2, z_lo: 4; z = z_hi * 4 + z_lo), core: 2. Of those that a mesh axis runs over, the one named last changes fastest.
Arguments:
- load_vectors: float32 [16, 16, 8, 8, 192], P('gx', 'gy'), may hold values from -45 to 45
- bond_stiffness: bfloat16 [16, 16, 8, 13, 36864], P('gx', 'gy'), may hold values from 0 to 0.0016937256
- intact_words: int32 [16, 16, 8, 13, 64, 4], P('gx', 'gy'), may hold values from 0 to 65535
- block_cols: int32 [16, 16, 8, 13], P('gx', 'gy'), may hold values from 0 to 89, as said below
- self_stiffness: bfloat16 [16, 16, 8, 36864], P('gx', 'gy'), may hold values from -0.01 to 3.01, as said below
- block_inverse: float32 [16, 16, 8, 36864], P('gx', 'gy'), may hold values from -0.01 to 0.61, as said below
- coarse_basis: float32 [16, 16, 16, 8, 192], P('gx', 'gy'), may hold values from -0.3 to 0.3
- coarse_factor: float32 [4096, 4096], P(('gx', 'gy')), may hold values from -0.375 to 0.375
Outputs:
- displacement: float32 [16, 16, 8, 8, 192], P('gx', 'gy')
- residual: float32 [16, 16, 8, 8, 192], P('gx', 'gy')
Inputs may be any that keep to these rules, and one draw needn't show every extreme that they name: `block_cols`: the 13 codes of a block name different blocks among the 26 around it (never the block itself), each |a - 1|, |c - 1|, |w - 1 - z| at most 1. `self_stiffness`: each block, read as a matrix, is symmetric. `block_inverse`: each block, read as a matrix, is symmetric.
All inputs are finite; a program needn't handle non-finite values.
Results may differ from a plain program's by a relative error of at most 0.0055.
Values may be sent and summed in bfloat16 or wider, within the bound.
No kernel may reach another device: no remote copies, remote signals or barrier semaphores. Data moves between devices by JAX's collectives and lax.ppermute only.
A program may use at most 128 MiB of HBM per device.

v0:
```python
import jax
import jax.numpy as jnp
from jax import lax
from jax.sharding import PartitionSpec as P

COMP = 3
PB = 64
DOF = 192
NS = 13
BZ = 8
NLOAD = 8
ITERS = 2


highest = lax.Precision.HIGHEST


def all_sum(x):
    for axis in ("gy", "gx"):
        size = lax.axis_size(axis)
        if size & (size - 1):
            x = lax.psum(x, axis)
            continue
        span = 1
        while span < size:
            pairs = [(i, i ^ span) for i in range(size)]
            x = x + lax.ppermute(x, axis, pairs)
            span *= 2
    return x


def padded_2(x, sides, width):
    for axis, dim in sides:
        size, length = (lax.axis_size(axis), x.shape[dim])
        up = [(i, (i + 1) % size) for i in range(size - 1)]
        down = [(j, i) for i, j in up]
        last = lax.slice_in_dim(x, length - width, length, axis=dim)
        initial = lax.slice_in_dim(x, 0, width, axis=dim)
        before = lax.ppermute(last, axis, up)
        after = lax.ppermute(initial, axis, down)
        x = jnp.concatenate([before, x, after], axis=dim)
    return x


def unpack_bits(packed):
    shifts = jnp.arange(16, dtype=jnp.int32)
    bitset = jnp.right_shift(packed[..., None], shifts) & 1
    return bitset.reshape(packed.shape[:-1] + (packed.shape[-1] * 16,))


def masked_blocks(stiffness, packed):
    intact = unpack_bits(packed).astype(stiffness.dtype)
    leading = stiffness.shape[:-1]
    spread = (
        jnp.arange(DOF, dtype=jnp.int32)[:, None] % PB == jnp.arange(PB, dtype=jnp.int32)[None, :]
    ).astype(stiffness.dtype)
    wide = jnp.einsum("Ii,...ij,Jj->...IJ", spread, intact, spread, preferred_element_type=jnp.float32)
    return stiffness.reshape(leading + (DOF, DOF)) * wide.astype(stiffness.dtype)


def per_device(
    load_vectors,
    bond_stiffness,
    intact_words,
    block_cols,
    self_stiffness,
    block_inverse,
    coarse_basis,
    coarse_factor,
):
    weights = masked_blocks(bond_stiffness[0, 0], intact_words[0, 0])
    row_total = jnp.sum(weights, axis=(1, 3), dtype=jnp.float32)
    column_total = jnp.sum(weights, axis=2, dtype=jnp.float32)
    col_codes = block_cols[0, 0]
    depth_span = BZ + 2
    ghost_count = 9 * depth_span
    selector = (
        jnp.arange(ghost_count, dtype=jnp.int32)[:, None] == col_codes.reshape(-1)[None, :]
    ).astype(jnp.bfloat16)
    self_block = self_stiffness[0, 0].reshape(BZ, DOF, DOF)
    inverse = block_inverse[0, 0].reshape(BZ, DOF, DOF)
    coarse_vecs = coarse_basis[0, 0]

    def precondition(residual):
        own_part = jnp.einsum("bij,blj->bli", inverse, residual, precision=highest)
        restricted = jnp.einsum("kbi,bli->lk", coarse_vecs, residual, precision=highest)
        coarse_term = jnp.dot(restricted, coarse_factor, precision=highest)
        local_energy = jnp.sum(residual * own_part, axis=(0, 2))
        summed = all_sum(jnp.concatenate([coarse_term, local_energy[:, None]], axis=1))
        coarse_sum = summed[:, :-1]
        spread = jnp.einsum("lc,kc->lk", coarse_sum, coarse_factor, precision=highest)
        smoothed = own_part + jnp.einsum("kbi,lk->bli", coarse_vecs, spread, precision=highest)
        energy = summed[:, -1] + jnp.sum(coarse_sum * coarse_sum, axis=1)
        return (smoothed, energy)

    residual = load_vectors[0, 0]
    solution = jnp.zeros_like(residual)
    smoothed, energy = precondition(residual)
    direction = smoothed
    for iteration in range(ITERS):
        rounded = direction.astype(jnp.bfloat16)
        ghosts = padded_2(rounded[None, None], (("gx", 0), ("gy", 1)), 1)
        padded = jnp.pad(ghosts, ((0, 0), (0, 0), (1, 1), (0, 0), (0, 0))).reshape(
            ghost_count, NLOAD, DOF
        )
        gathered = jnp.take(padded, col_codes, axis=0)
        forward = row_total[:, None, :] * rounded - jnp.einsum(
            "bsij,bslj->bli", weights, gathered, preferred_element_type=jnp.float32
        )
        backward = column_total[:, :, None, :] * gathered - jnp.einsum(
            "bsij,bli->bslj", weights, rounded, preferred_element_type=jnp.float32
        )
        flat_terms = backward.reshape(BZ * NS, NLOAD * DOF)
        high_part = flat_terms.astype(jnp.bfloat16)
        low_part = (flat_terms - high_part.astype(jnp.float32)).astype(jnp.bfloat16)
        apply_spread = jnp.dot(selector, high_part, preferred_element_type=jnp.float32) + jnp.dot(
            selector, low_part, preferred_element_type=jnp.float32
        )
        partial_value = apply_spread.reshape(3, 3, depth_span, NLOAD, DOF)[:, :, 1 : depth_span - 1]
        beside_all = padded_2(partial_value.astype(jnp.bfloat16), (("gx", 0), ("gy", 1)), 1).astype(
            partial_value.dtype
        )
        folded = (
            beside_all[2, 2]
            + beside_all[0, 0]
            + beside_all[0, 2]
            + beside_all[0, 4]
            + beside_all[2, 0]
        )
        folded = folded + beside_all[2, 4] + beside_all[4, 0] + beside_all[4, 2] + beside_all[4, 4]
        diagonal = jnp.einsum(
            "bij,blj->bli", self_block, rounded, preferred_element_type=jnp.float32
        )
        operator_out = diagonal + forward + folded
        curve_sum = all_sum(jnp.sum(direction * operator_out, axis=(0, 2)))
        step_scale = (energy / curve_sum)[None, :, None]
        solution = solution + step_scale * direction
        residual = residual - step_scale * operator_out
        if iteration + 1 < ITERS:
            smoothed, new_energy = precondition(residual)
            direction = smoothed + (new_energy / energy)[None, :, None] * direction
            energy = new_energy
    return (solution[None, None], residual[None, None])


def solution(mesh):
    in_specs = (
        P("gx", "gy", None, None, None),
        P("gx", "gy", None, None, None),
        P("gx", "gy", None, None, None, None),
        P("gx", "gy", None, None),
        P("gx", "gy", None, None),
        P("gx", "gy", None, None),
        P("gx", "gy", None, None, None),
        P(("gx", "gy"), None),
    )
    out_specs = (P("gx", "gy", None, None, None), P("gx", "gy", None, None, None))
    return jax.shard_map(
        per_device, mesh=mesh, in_specs=in_specs, out_specs=out_specs, check_vma=False
    )
```

profile of v0, /device:TPU:14, one launch (start us, length us, event | category | flops | bytes accessed | tf_op | source)
XLA Modules:
  0.0 348.8 jit_solution(16737628911366942337)
XLA Ops:
  8.1 7.3 %collective-permute-start.1 = (f32[8,4097]{1,0:T(8,128)S(1)}, f32[8,4097]{1,0:T(8,128)S(1)}, u32[]{:S(2)}, u32[]{:S(2)}) collective-permute-start(f32[8,4097]{1,0:T(8,128)S(1)} %fusion.59), channel_id=1, source_target_pairs={{0,2},{1,3},{2,0},{3,1},{4,6},{5,7},{6,4},{7,5},{8,10},{9,11},{10,... | collective-permute-start | bytes 393320 | tf_op jit(solution)/shard_map/ppermute | solution.py:27
  15.4 4.0 %collective-permute-done.1 = f32[8,4097]{1,0:T(8,128)S(1)} collective-permute-done((f32[8,4097]{1,0:T(8,128)S(1)}, f32[8,4097]{1,0:T(8,128)S(1)}, u32[]{:S(2)}, u32[]{:S(2)}) %collective-permute-start.1) | collective-permute-done | bytes 131136 | tf_op jit(solution)/shard_map/ppermute | solution.py:27
  20.4 4.2 %collective-permute-done.2 = f32[8,4097]{1,0:T(8,128)S(1)} collective-permute-done((f32[8,4097]{1,0:T(8,128)S(1)}, f32[8,4097]{1,0:T(8,128)S(1)}, u32[]{:S(2)}, u32[]{:S(2)}) %collective-permute-start.2) | collective-permute-done | bytes 131136 | tf_op jit(solution)/shard_map/ppermute | solution.py:27
  26.1 5.1 %collective-permute-done.3 = f32[8,4097]{1,0:T(8,128)S(1)} collective-permute-done((f32[8,4097]{1,0:T(8,128)S(1)}, f32[8,4097]{1,0:T(8,128)S(1)}, u32[]{:S(2)}, u32[]{:S(2)}) %collective-permute-start.3) | collective-permute-done | bytes 131136 | tf_op jit(solution)/shard_map/ppermute | solution.py:27
  31.2 3.9 %collective-permute-start.4 = (f32[8,4097]{1,0:T(8,128)S(1)}, f32[8,4097]{1,0:T(8,128)S(1)}, u32[]{:S(2)}, u32[]{:S(2)}) collective-permute-start(f32[8,4097]{1,0:T(8,128)S(1)} %add.226), channel_id=1, source_target_pairs={{0,16},{16,0},{32,48},{48,32},{64,80},{80,64},{96,112},{112,96},{1... | collective-permute-start | bytes 393320 | tf_op jit(solution)/shard_map/ppermute | solution.py:27
  35.1 3.2 collective-permute-done.4
  38.4 3.8 %collective-permute-start.5 = (f32[8,4097]{1,0:T(8,128)S(1)}, f32[8,4097]{1,0:T(8,128)S(1)}, u32[]{:S(2)}, u32[]{:S(2)}) collective-permute-start(f32[8,4097]{1,0:T(8,128)S(1)} %add.227), channel_id=1, source_target_pairs={{0,32},{16,48},{32,0},{48,16},{64,96},{80,112},{96,64},{112,80},{1... | collective-permute-start | bytes 393320 | tf_op jit(solution)/shard_map/ppermute | solution.py:27
  42.3 16.6 %reshape_squeeze.11 = bf16[8,13,192,192]{3,2,0,1:T(8,128)(2,1)} reshape(bf16[1,1,8,13,36864]{4,2,3,1,0:T(8,128)(2,1)} %param.11) | data formatting | bytes 15335424 | tf_op jit(solution)/shard_map/reshape;squeeze | solution.py:58
  61.4 10.8 %convert_reduce_fusion.1 = (f32[8,192]{1,0:T(8,128)S(1)}, f32[8,13,192]{2,1,0:T(8,128)S(1)}, bf16[8,13,192,192]{3,2,1,0:T(8,128)(2,1)}) fusion(s32[192]{0:T(256)S(1)} %and_select_fusion, bf16[8,13,64,64]{2,3,1,0:T(8,128)(2,1)} %fusion.1, bf16[8,13,192,192]{3,2,0,1:T(8,128)(2,1)} %reshape_squeeze.11), kind=kOutput, calls=%fused_computation.3 | convolution fusion | flops 684985344 | bytes 16274176 | tf_op jit(solution)/shard_map/Ii,...ij,Jj->...IJ/dot_general | solution.py:57
  74.9 3.9 %collective-permute-done.7 = f32[8,4097]{1,0:T(8,128)S(1)} collective-permute-done((f32[8,4097]{1,0:T(8,128)S(1)}, f32[8,4097]{1,0:T(8,128)S(1)}, u32[]{:S(2)}, u32[]{:S(2)}) %collective-permute-start.7) | collective-permute-done | bytes 131136 | tf_op jit(solution)/shard_map/ppermute | solution.py:27
  79.5 4.0 %collective-permute-start.9 = (bf16[1,1,8,8,192]{4,3,2,1,0:T(8,128)(2,1)S(1)}, bf16[1,1,8,8,192]{4,3,2,1,0:T(8,128)(2,1)S(1)}, u32[]{:S(2)}, u32[]{:S(2)}) collective-permute-start(bf16[1,1,8,8,192]{4,3,2,1,0:T(8,128)(2,1)S(1)} %bitcast.152), channel_id=1, source_target_pairs={{16,0},{32,16},{48,32},{64,48},{80,64},{96,80},{112,96},{128,112},... | collective-permute-start | bytes 73736 | tf_op jit(solution)/shard_map/ppermute | solution.py:40
  87.9 4.1 %collective-permute-done.8 = bf16[1,1,8,8,192]{4,3,2,1,0:T(8,128)(2,1)S(1)} collective-permute-done((bf16[1,1,8,8,192]{4,3,2,1,0:T(8,128)(2,1)S(1)}, bf16[1,1,8,8,192]{4,3,2,1,0:T(8,128)(2,1)S(1)}, u32[]{:S(2)}, u32[]{:S(2)}) %collective-permute-start.8) | collective-permute-done | bytes 24608 | tf_op jit(solution)/shard_map/ppermute | solution.py:39
  97.1 8.1 %collective-permute-done.10 = bf16[3,1,8,8,192]{4,3,2,1,0:T(8,128)(2,1)S(1)} collective-permute-done((bf16[3,1,8,8,192]{4,3,2,1,0:T(8,128)(2,1)S(1)}, bf16[3,1,8,8,192]{4,3,2,1,0:T(8,128)(2,1)S(1)}, u32[]{:S(2)}, u32[]{:S(2)}) %collective-permute-start.10) | collective-permute-done | bytes 73760 | tf_op jit(solution)/shard_map/ppermute | solution.py:39
  108.4 6.3 %fusion.7 = f32[8,13,8,192]{3,2,1,0:T(8,128)} fusion(bf16[8,13,192,192]{3,2,1,0:T(8,128)(2,1)} %get-tuple-element.23, f32[8,13,192]{2,1,0:T(8,128)S(1)} %get-tuple-element.4, bf16[8,13,8,192]{3,2,1,0:T(8,128)(2,1)S(1)} %bitcast.144, pred[8,13]{1,0:T(8,128)(4,1)S(1)} %compare_and_fusion, bf16[8,8,192]{2,1,0:T(8,128)(2,1)S(1)} %get-tuple-element.21), kind=kOutput, calls=%fused_computation.16 | convolution fusion | flops 61980672 | bytes 8730728 | tf_op jit(solution)/shard_map/bsij,bli->bslj/dot_general | solution.py:110
  120.6 3.9 %collective-permute-start.12 = (bf16[1,3,8,8,192]{4,3,2,1,0:T(8,128)(2,1)S(1)}, bf16[1,3,8,8,192]{4,3,2,1,0:T(8,128)(2,1)S(1)}, u32[]{:S(2)}, u32[]{:S(2)}) collective-permute-start(bf16[1,3,8,8,192]{4,3,2,1,0:T(8,128)(2,1)S(1)} %get-tuple-element.15), channel_id=1, source_target_pairs={{0,16},{16,32},{32,48},{48,64},{64,80},{80,96},{96,112},{112,128},... | collective-permute-start | bytes 221192 | tf_op jit(solution)/shard_map/ppermute | solution.py:39
  125.1 4.7 %collective-permute-done.12 = bf16[1,3,8,8,192]{4,3,2,1,0:T(8,128)(2,1)S(1)} collective-permute-done((bf16[1,3,8,8,192]{4,3,2,1,0:T(8,128)(2,1)S(1)}, bf16[1,3,8,8,192]{4,3,2,1,0:T(8,128)(2,1)S(1)}, u32[]{:S(2)}, u32[]{:S(2)}) %collective-permute-start.12) | collective-permute-done | bytes 73760 | tf_op jit(solution)/shard_map/ppermute | solution.py:39
  136.4 8.6 %collective-permute-done.14 = bf16[5,1,8,8,192]{4,3,2,1,0:T(8,128)(2,1)S(1)} collective-permute-done((bf16[5,1,8,8,192]{4,3,2,1,0:T(8,128)(2,1)S(1)}, bf16[5,1,8,8,192]{4,3,2,1,0:T(8,128)(2,1)S(1)}, u32[]{:S(2)}, u32[]{:S(2)}) %collective-permute-start.14) | collective-permute-done | bytes 122912 | tf_op jit(solution)/shard_map/ppermute | solution.py:39
  145.0 6.9 %multiply_reduce_fusion.4 = (f32[8]{0:T(128)S(1)}, f32[8,8,192]{2,1,0:T(8,128)S(1)}) fusion(f32[8,8,192]{2,1,0:T(8,128)S(1)} %get-tuple-element.22, bf16[5,1,8,8,192]{4,3,2,1,0:T(8,128)(2,1)S(1)} %collective-permute-done.15, bf16[1,3,8,8,192]{4,3,2,1,0:T(8,128)(2,1)S(1)} %collective-permute-done.13, bf16[3,3,8,8,192]{4,3,2,1,0:T(8,128)(2,1)S(1)} %slice.141, ...), kind=kOutput, calls=%fused_computation.106 | convolution fusion | flops 62238712 | bytes 8779912 | tf_op jit(solution)/shard_map/bsij,bslj->bli/dot_general | solution.py:107
  155.7 5.0 %collective-permute-done.17 = f32[8]{0:T(128)S(1)} collective-permute-done((f32[8]{0:T(128)S(1)}, f32[8]{0:T(128)S(1)}, u32[]{:S(2)}, u32[]{:S(2)}) %collective-permute-start.17) | collective-permute-done | bytes 64 | tf_op jit(solution)/shard_map/ppermute | solution.py:27
  161.5 2.8 collective-permute-done.18
  165.0 4.3 %collective-permute-done.19 = f32[8]{0:T(128)S(1)} collective-permute-done((f32[8]{0:T(128)S(1)}, f32[8]{0:T(128)S(1)}, u32[]{:S(2)}, u32[]{:S(2)}) %collective-permute-start.19) | collective-permute-done | bytes 64 | tf_op jit(solution)/shard_map/ppermute | solution.py:27
  169.3 3.6 %collective-permute-done.20 = f32[8]{0:T(128)S(1)} collective-permute-done((f32[8]{0:T(128)S(1)}, f32[8]{0:T(128)S(1)}, u32[]{:S(2)}, u32[]{:S(2)}) %collective-permute-start.20) | collective-permute-done | bytes 64 | tf_op jit(solution)/shard_map/ppermute | solution.py:27
  172.9 4.5 %collective-permute-done.21 = f32[8]{0:T(128)S(1)} collective-permute-done((f32[8]{0:T(128)S(1)}, f32[8]{0:T(128)S(1)}, u32[]{:S(2)}, u32[]{:S(2)}) %collective-permute-start.21) | collective-permute-done | bytes 64 | tf_op jit(solution)/shard_map/ppermute | solution.py:27
  177.4 3.6 %collective-permute-done.22 = f32[8]{0:T(128)S(1)} collective-permute-done((f32[8]{0:T(128)S(1)}, f32[8]{0:T(128)S(1)}, u32[]{:S(2)}, u32[]{:S(2)}) %collective-permute-start.22) | collective-permute-done | bytes 64 | tf_op jit(solution)/shard_map/ppermute | solution.py:27
  183.3 2.8 collective-permute-done.23
  190.6 12.2 %collective-permute-start.25 = (f32[8,4097]{1,0:T(8,128)S(1)}, f32[8,4097]{1,0:T(8,128)S(1)}, u32[]{:S(2)}, u32[]{:S(2)}) collective-permute-start(f32[8,4097]{1,0:T(8,128)S(1)} %fusion.58), channel_id=1, source_target_pairs={{0,2},{1,3},{2,0},{3,1},{4,6},{5,7},{6,4},{7,5},{8,10},{9,11},{10,... | collective-permute-start | bytes 393320 | tf_op jit(solution)/shard_map/ppermute | solution.py:27
  202.8 9.5 %collective-permute-done.25 = f32[8,4097]{1,0:T(8,128)S(1)} collective-permute-done((f32[8,4097]{1,0:T(8,128)S(1)}, f32[8,4097]{1,0:T(8,128)S(1)}, u32[]{:S(2)}, u32[]{:S(2)}) %collective-permute-start.25) | collective-permute-done | bytes 131136 | tf_op jit(solution)/shard_map/ppermute | solution.py:27
  213.6 4.3 %collective-permute-done.26 = f32[8,4097]{1,0:T(8,128)S(1)} collective-permute-done((f32[8,4097]{1,0:T(8,128)S(1)}, f32[8,4097]{1,0:T(8,128)S(1)}, u32[]{:S(2)}, u32[]{:S(2)}) %collective-permute-start.26) | collective-permute-done | bytes 131136 | tf_op jit(solution)/shard_map/ppermute | solution.py:27
  218.7 5.8 %collective-permute-done.27 = f32[8,4097]{1,0:T(8,128)S(1)} collective-permute-done((f32[8,4097]{1,0:T(8,128)S(1)}, f32[8,4097]{1,0:T(8,128)S(1)}, u32[]{:S(2)}, u32[]{:S(2)}) %collective-permute-start.27) | collective-permute-done | bytes 131136 | tf_op jit(solution)/shard_map/ppermute | solution.py:27
  224.7 5.0 %collective-permute-done.28 = f32[8,4097]{1,0:T(8,128)S(1)} collective-permute-done((f32[8,4097]{1,0:T(8,128)S(1)}, f32[8,4097]{1,0:T(8,128)S(1)}, u32[]{:S(2)}, u32[]{:S(2)}) %collective-permute-start.28) | collective-permute-done | bytes 131136 | tf_op jit(solution)/shard_map/ppermute | solution.py:27
  229.8 6.9 %collective-permute-done.29 = f32[8,4097]{1,0:T(8,128)S(1)} collective-permute-done((f32[8,4097]{1,0:T(8,128)S(1)}, f32[8,4097]{1,0:T(8,128)S(1)}, u32[]{:S(2)}, u32[]{:S(2)}) %collective-permute-start.29) | collective-permute-done | bytes 131136 | tf_op jit(solution)/shard_map/ppermute | solution.py:27
  237.3 6.0 %collective-permute-done.30 = f32[8,4097]{1,0:T(8,128)S(1)} collective-permute-done((f32[8,4097]{1,0:T(8,128)S(1)}, f32[8,4097]{1,0:T(8,128)S(1)}, u32[]{:S(2)}, u32[]{:S(2)}) %collective-permute-start.30) | collective-permute-done | bytes 131136 | tf_op jit(solution)/shard_map/ppermute | solution.py:27
  244.1 5.7 %collective-permute-done.31 = f32[8,4097]{1,0:T(8,128)S(1)} collective-permute-done((f32[8,4097]{1,0:T(8,128)S(1)}, f32[8,4097]{1,0:T(8,128)S(1)}, u32[]{:S(2)}, u32[]{:S(2)}) %collective-permute-start.31) | collective-permute-done | bytes 131136 | tf_op jit(solution)/shard_map/ppermute | solution.py:27
  252.7 3.9 %collective-permute-start.32 = (bf16[1,1,8,8,192]{4,3,2,1,0:T(8,128)(2,1)S(1)}, bf16[1,1,8,8,192]{4,3,2,1,0:T(8,128)(2,1)S(1)}, u32[]{:S(2)}, u32[]{:S(2)}) collective-permute-start(bf16[1,1,8,8,192]{4,3,2,1,0:T(8,128)(2,1)S(1)} %bitcast.157), channel_id=1, source_target_pairs={{0,16},{16,32},{32,48},{48,64},{64,80},{80,96},{96,112},{112,128},... | collective-permute-start | bytes 73736 | tf_op jit(solution)/shard_map/ppermute | solution.py:39
  256.7 4.6 %collective-permute-done.32 = bf16[1,1,8,8,192]{4,3,2,1,0:T(8,128)(2,1)S(1)} collective-permute-done((bf16[1,1,8,8,192]{4,3,2,1,0:T(8,128)(2,1)S(1)}, bf16[1,1,8,8,192]{4,3,2,1,0:T(8,128)(2,1)S(1)}, u32[]{:S(2)}, u32[]{:S(2)}) %collective-permute-start.32) | collective-permute-done | bytes 24608 | tf_op jit(solution)/shard_map/ppermute | solution.py:39
  265.6 8.3 %collective-permute-done.34 = bf16[3,1,8,8,192]{4,3,2,1,0:T(8,128)(2,1)S(1)} collective-permute-done((bf16[3,1,8,8,192]{4,3,2,1,0:T(8,128)(2,1)S(1)}, bf16[3,1,8,8,192]{4,3,2,1,0:T(8,128)(2,1)S(1)}, u32[]{:S(2)}, u32[]{:S(2)}) %collective-permute-start.34) | collective-permute-done | bytes 73760 | tf_op jit(solution)/shard_map/ppermute | solution.py:39
  274.6 5.3 %fusion.6 = f32[8,13,8,192]{3,2,1,0:T(8,128)S(1)} fusion(bf16[8,13,192,192]{3,2,1,0:T(8,128)(2,1)} %get-tuple-element.23, f32[8,13,192]{2,1,0:T(8,128)} %copy-done.6, bf16[8,13,8,192]{3,2,1,0:T(8,128)(2,1)S(1)} %bitcast.142, pred[8,13]{1,0:T(8,128)(4,1)S(1)} %compare_and_fusion, bf16[8,8,192]{2,1,0:T(8,128)(2,1)S(1)} %get-tuple-element.28), kind=kOutput, calls=%fused_computation.14 | convolution fusion | flops 61980672 | bytes 8730728 | tf_op jit(solution)/shard_map/bsij,bli->bslj/dot_general | solution.py:110
  283.0 3.9 %collective-permute-start.36 = (bf16[1,3,8,8,192]{4,3,2,1,0:T(8,128)(2,1)S(1)}, bf16[1,3,8,8,192]{4,3,2,1,0:T(8,128)(2,1)S(1)}, u32[]{:S(2)}, u32[]{:S(2)}) collective-permute-start(bf16[1,3,8,8,192]{4,3,2,1,0:T(8,128)(2,1)S(1)} %get-tuple-element.13), channel_id=1, source_target_pairs={{0,16},{16,32},{32,48},{48,64},{64,80},{80,96},{96,112},{112,128},... | collective-permute-start | bytes 221192 | tf_op jit(solution)/shard_map/ppermute | solution.py:39
  287.9 4.4 %collective-permute-done.36 = bf16[1,3,8,8,192]{4,3,2,1,0:T(8,128)(2,1)S(1)} collective-permute-done((bf16[1,3,8,8,192]{4,3,2,1,0:T(8,128)(2,1)S(1)}, bf16[1,3,8,8,192]{4,3,2,1,0:T(8,128)(2,1)S(1)}, u32[]{:S(2)}, u32[]{:S(2)}) %collective-permute-start.36) | collective-permute-done | bytes 73760 | tf_op jit(solution)/shard_map/ppermute | solution.py:39
  297.1 9.9 %collective-permute-done.38 = bf16[5,1,8,8,192]{4,3,2,1,0:T(8,128)(2,1)S(1)} collective-permute-done((bf16[5,1,8,8,192]{4,3,2,1,0:T(8,128)(2,1)S(1)}, bf16[5,1,8,8,192]{4,3,2,1,0:T(8,128)(2,1)S(1)}, u32[]{:S(2)}, u32[]{:S(2)}) %collective-permute-start.38) | collective-permute-done | bytes 122912 | tf_op jit(solution)/shard_map/ppermute | solution.py:39
  307.0 6.8 %multiply_reduce_fusion.2 = (f32[8]{0:T(128)S(1)}, f32[8,8,192]{2,1,0:T(8,128)S(1)}) fusion(f32[8,8,192]{2,1,0:T(8,128)S(1)} %get-tuple-element.29, bf16[5,1,8,8,192]{4,3,2,1,0:T(8,128)(2,1)S(1)} %collective-permute-done.39, bf16[1,3,8,8,192]{4,3,2,1,0:T(8,128)(2,1)S(1)} %collective-permute-done.37, bf16[3,3,8,8,192]{4,3,2,1,0:T(8,128)(2,1)S(1)} %slice.146, ...), kind=kOutput, calls=%fused_computation.104 | convolution fusion | flops 62238712 | bytes 8779912 | tf_op jit(solution)/shard_map/bsij,bslj->bli/dot_general | solution.py:107
  315.0 7.5 %collective-permute-done.41 = f32[8]{0:T(128)S(1)} collective-permute-done((f32[8]{0:T(128)S(1)}, f32[8]{0:T(128)S(1)}, u32[]{:S(2)}, u32[]{:S(2)}) %collective-permute-start.41) | collective-permute-done | bytes 64 | tf_op jit(solution)/shard_map/ppermute | solution.py:27
  323.0 3.1 collective-permute-done.42
  326.1 5.1 %collective-permute-done.43 = f32[8]{0:T(128)S(1)} collective-permute-done((f32[8]{0:T(128)S(1)}, f32[8]{0:T(128)S(1)}, u32[]{:S(2)}, u32[]{:S(2)}) %collective-permute-start.43) | collective-permute-done | bytes 64 | tf_op jit(solution)/shard_map/ppermute | solution.py:27
  331.2 3.6 %collective-permute-done.44 = f32[8]{0:T(128)S(1)} collective-permute-done((f32[8]{0:T(128)S(1)}, f32[8]{0:T(128)S(1)}, u32[]{:S(2)}, u32[]{:S(2)}) %collective-permute-start.44) | collective-permute-done | bytes 64 | tf_op jit(solution)/shard_map/ppermute | solution.py:27
  334.8 4.5 %collective-permute-done.45 = f32[8]{0:T(128)S(1)} collective-permute-done((f32[8]{0:T(128)S(1)}, f32[8]{0:T(128)S(1)}, u32[]{:S(2)}, u32[]{:S(2)}) %collective-permute-start.45) | collective-permute-done | bytes 64 | tf_op jit(solution)/shard_map/ppermute | solution.py:27
  339.2 3.6 %collective-permute-done.46 = f32[8]{0:T(128)S(1)} collective-permute-done((f32[8]{0:T(128)S(1)}, f32[8]{0:T(128)S(1)}, u32[]{:S(2)}, u32[]{:S(2)}) %collective-permute-start.46) | collective-permute-done | bytes 64 | tf_op jit(solution)/shard_map/ppermute | solution.py:27
  344.3 3.6 %collective-permute-done.47 = f32[8]{0:T(128)S(1)} collective-permute-done((f32[8]{0:T(128)S(1)}, f32[8]{0:T(128)S(1)}, u32[]{:S(2)}, u32[]{:S(2)}) %collective-permute-start.47) | collective-permute-done | bytes 64 | tf_op jit(solution)/shard_map/ppermute | solution.py:27
  (162 shorter events, 78.1 us)
Async XLA Ops:
  6.7 1.4 collective-permute-start
  8.1 11.3 %collective-permute-start.1 = (f32[8,4097]{1,0:T(8,128)S(1)}, f32[8,4097]{1,0:T(8,128)S(1)}, u32[]{:S(2)}, u32[]{:S(2)}) collective-permute-start(f32[8,4097]{1,0:T(8,128)S(1)} %fusion.59), channel_id=1, source_target_pairs={{0,2},{1,3},{2,0},{3,1},{4,6},{5,7},{6,4},{7,5},{8,10},{9,11},{10,... | collective-permute-start | bytes 393320 | tf_op jit(solution)/shard_map/ppermute | solution.py:27
  19.4 5.1 %collective-permute-start.2 = (f32[8,4097]{1,0:T(8,128)S(1)}, f32[8,4097]{1,0:T(8,128)S(1)}, u32[]{:S(2)}, u32[]{:S(2)}) collective-permute-start(f32[8,4097]{1,0:T(8,128)S(1)} %add.224), channel_id=1, source_target_pairs={{0,4},{1,5},{2,6},{3,7},{4,0},{5,1},{6,2},{7,3},{8,12},{9,13},{10,... | collective-permute-start | bytes 393320 | tf_op jit(solution)/shard_map/ppermute | solution.py:27
  24.6 6.6 %collective-permute-start.3 = (f32[8,4097]{1,0:T(8,128)S(1)}, f32[8,4097]{1,0:T(8,128)S(1)}, u32[]{:S(2)}, u32[]{:S(2)}) collective-permute-start(f32[8,4097]{1,0:T(8,128)S(1)} %add.225), channel_id=1, source_target_pairs={{0,8},{1,9},{2,10},{3,11},{4,12},{5,13},{6,14},{7,15},{8,0},{9,1},... | collective-permute-start | bytes 393320 | tf_op jit(solution)/shard_map/ppermute | solution.py:27
  31.2 7.2 %collective-permute-start.4 = (f32[8,4097]{1,0:T(8,128)S(1)}, f32[8,4097]{1,0:T(8,128)S(1)}, u32[]{:S(2)}, u32[]{:S(2)}) collective-permute-start(f32[8,4097]{1,0:T(8,128)S(1)} %add.226), channel_id=1, source_target_pairs={{0,16},{16,0},{32,48},{48,32},{64,80},{80,64},{96,112},{112,96},{1... | collective-permute-start | bytes 393320 | tf_op jit(solution)/shard_map/ppermute | solution.py:27
  38.4 22.4 %collective-permute-start.5 = (f32[8,4097]{1,0:T(8,128)S(1)}, f32[8,4097]{1,0:T(8,128)S(1)}, u32[]{:S(2)}, u32[]{:S(2)}) collective-permute-start(f32[8,4097]{1,0:T(8,128)S(1)} %add.227), channel_id=1, source_target_pairs={{0,32},{16,48},{32,0},{48,16},{64,96},{80,112},{96,64},{112,80},{1... | collective-permute-start | bytes 393320 | tf_op jit(solution)/shard_map/ppermute | solution.py:27
  60.8 11.3 %collective-permute-start.6 = (f32[8,4097]{1,0:T(8,128)S(1)}, f32[8,4097]{1,0:T(8,128)S(1)}, u32[]{:S(2)}, u32[]{:S(2)}) collective-permute-start(f32[8,4097]{1,0:T(8,128)S(1)} %add.228), channel_id=1, source_target_pairs={{0,64},{16,80},{32,96},{48,112},{64,0},{80,16},{96,32},{112,48},{1... | collective-permute-start | bytes 393320 | tf_op jit(solution)/shard_map/ppermute | solution.py:27
  72.2 6.6 %collective-permute-start.7 = (f32[8,4097]{1,0:T(8,128)S(1)}, f32[8,4097]{1,0:T(8,128)S(1)}, u32[]{:S(2)}, u32[]{:S(2)}) collective-permute-start(f32[8,4097]{1,0:T(8,128)S(1)} %add.229), channel_id=1, source_target_pairs={{0,128},{16,144},{32,160},{48,176},{64,192},{80,208},{96,224},{112... | collective-permute-start | bytes 393320 | tf_op jit(solution)/shard_map/ppermute | solution.py:27
  79.5 8.4 %collective-permute-start.9 = (bf16[1,1,8,8,192]{4,3,2,1,0:T(8,128)(2,1)S(1)}, bf16[1,1,8,8,192]{4,3,2,1,0:T(8,128)(2,1)S(1)}, u32[]{:S(2)}, u32[]{:S(2)}) collective-permute-start(bf16[1,1,8,8,192]{4,3,2,1,0:T(8,128)(2,1)S(1)} %bitcast.152), channel_id=1, source_target_pairs={{16,0},{32,16},{48,32},{64,48},{80,64},{96,80},{112,96},{128,112},... | collective-permute-start | bytes 73736 | tf_op jit(solution)/shard_map/ppermute | solution.py:40
  83.5 8.5 %collective-permute-start.8 = (bf16[1,1,8,8,192]{4,3,2,1,0:T(8,128)(2,1)S(1)}, bf16[1,1,8,8,192]{4,3,2,1,0:T(8,128)(2,1)S(1)}, u32[]{:S(2)}, u32[]{:S(2)}) collective-permute-start(bf16[1,1,8,8,192]{4,3,2,1,0:T(8,128)(2,1)S(1)} %bitcast.153), channel_id=1, source_target_pairs={{0,16},{16,32},{32,48},{48,64},{64,80},{80,96},{96,112},{112,128},... | collective-permute-start | bytes 73736 | tf_op jit(solution)/shard_map/ppermute | solution.py:39
  92.0 5.1 %collective-permute-start.11 = (bf16[3,1,8,8,192]{4,3,2,1,0:T(8,128)(2,1)S(1)}, bf16[3,1,8,8,192]{4,3,2,1,0:T(8,128)(2,1)S(1)}, u32[]{:S(2)}, u32[]{:S(2)}) collective-permute-start(bf16[3,1,8,8,192]{4,3,2,1,0:T(8,128)(2,1)S(1)} %pad_maximum_fusion.8), channel_id=1, source_target_pairs={{1,0},{2,1},{3,2},{4,3},{5,4},{6,5},{7,6},{8,7},{9,8},{10,9},{11,1... | collective-permute-start | bytes 221192 | tf_op jit(solution)/shard_map/ppermute | solution.py:40
  94.0 11.3 %collective-permute-start.10 = (bf16[3,1,8,8,192]{4,3,2,1,0:T(8,128)(2,1)S(1)}, bf16[3,1,8,8,192]{4,3,2,1,0:T(8,128)(2,1)S(1)}, u32[]{:S(2)}, u32[]{:S(2)}) collective-permute-start(bf16[3,1,8,8,192]{4,3,2,1,0:T(8,128)(2,1)S(1)} %pad_maximum_fusion.8), channel_id=1, source_target_pairs={{0,1},{1,2},{2,3},{3,4},{4,5},{5,6},{6,7},{7,8},{8,9},{9,10},{10,1... | collective-permute-start | bytes 221192 | tf_op jit(solution)/shard_map/ppermute | solution.py:39
  118.6 6.5 %collective-permute-start.13 = (bf16[1,3,8,8,192]{4,3,2,1,0:T(8,128)(2,1)S(1)}, bf16[1,3,8,8,192]{4,3,2,1,0:T(8,128)(2,1)S(1)}, u32[]{:S(2)}, u32[]{:S(2)}) collective-permute-start(bf16[1,3,8,8,192]{4,3,2,1,0:T(8,128)(2,1)S(1)} %get-tuple-element.16), channel_id=1, source_target_pairs={{16,0},{32,16},{48,32},{64,48},{80,64},{96,80},{112,96},{128,112},... | collective-permute-start | bytes 221192 | tf_op jit(solution)/shard_map/ppermute | solution.py:40
  120.6 9.3 %collective-permute-start.12 = (bf16[1,3,8,8,192]{4,3,2,1,0:T(8,128)(2,1)S(1)}, bf16[1,3,8,8,192]{4,3,2,1,0:T(8,128)(2,1)S(1)}, u32[]{:S(2)}, u32[]{:S(2)}) collective-permute-start(bf16[1,3,8,8,192]{4,3,2,1,0:T(8,128)(2,1)S(1)} %get-tuple-element.15), channel_id=1, source_target_pairs={{0,16},{16,32},{32,48},{48,64},{64,80},{80,96},{96,112},{112,128},... | collective-permute-start | bytes 221192 | tf_op jit(solution)/shard_map/ppermute | solution.py:39
  129.9 6.5 %collective-permute-start.15 = (bf16[5,1,8,8,192]{4,3,2,1,0:T(8,128)(2,1)S(1)}, bf16[5,1,8,8,192]{4,3,2,1,0:T(8,128)(2,1)S(1)}, u32[]{:S(2)}, u32[]{:S(2)}) collective-permute-start(bf16[5,1,8,8,192]{4,3,2,1,0:T(8,128)(2,1)S(1)} %get-tuple-element.12), channel_id=1, source_target_pairs={{1,0},{2,1},{3,2},{4,3},{5,4},{6,5},{7,6},{8,7},{9,8},{10,9},{11,1... | collective-permute-start | bytes 368648 | tf_op jit(solution)/shard_map/ppermute | solution.py:40
  131.8 13.2 %collective-permute-start.14 = (bf16[5,1,8,8,192]{4,3,2,1,0:T(8,128)(2,1)S(1)}, bf16[5,1,8,8,192]{4,3,2,1,0:T(8,128)(2,1)S(1)}, u32[]{:S(2)}, u32[]{:S(2)}) collective-permute-start(bf16[5,1,8,8,192]{4,3,2,1,0:T(8,128)(2,1)S(1)} %get-tuple-element.11), channel_id=1, source_target_pairs={{0,1},{1,2},{2,3},{3,4},{4,5},{5,6},{6,7},{7,8},{8,9},{9,10},{10,1... | collective-permute-start | bytes 368648 | tf_op jit(solution)/shard_map/ppermute | solution.py:39
  152.0 1.2 collective-permute-start.16
  153.2 7.5 %collective-permute-start.17 = (f32[8]{0:T(128)S(1)}, f32[8]{0:T(128)S(1)}, u32[]{:S(2)}, u32[]{:S(2)}) collective-permute-start(f32[8]{0:T(128)S(1)} %add.246), channel_id=1, source_target_pairs={{0,2},{1,3},{2,0},{3,1},{4,6},{5,7},{6,4},{7,5},{8,10},{9,11},{10,... | collective-permute-start | bytes 104 | tf_op jit(solution)/shard_map/ppermute | solution.py:27
  160.7 3.6 %collective-permute-start.18 = (f32[8]{0:T(128)S(1)}, f32[8]{0:T(128)S(1)}, u32[]{:S(2)}, u32[]{:S(2)}) collective-permute-start(f32[8]{0:T(128)S(1)} %add.247), channel_id=1, source_target_pairs={{0,4},{1,5},{2,6},{3,7},{4,0},{5,1},{6,2},{7,3},{8,12},{9,13},{10,... | collective-permute-start | bytes 104 | tf_op jit(solution)/shard_map/ppermute | solution.py:27
  164.3 5.1 %collective-permute-start.19 = (f32[8]{0:T(128)S(1)}, f32[8]{0:T(128)S(1)}, u32[]{:S(2)}, u32[]{:S(2)}) collective-permute-start(f32[8]{0:T(128)S(1)} %add.248), channel_id=1, source_target_pairs={{0,8},{1,9},{2,10},{3,11},{4,12},{5,13},{6,14},{7,15},{8,0},{9,1},... | collective-permute-start | bytes 104 | tf_op jit(solution)/shard_map/ppermute | solution.py:27
  169.3 3.6 %collective-permute-start.20 = (f32[8]{0:T(128)S(1)}, f32[8]{0:T(128)S(1)}, u32[]{:S(2)}, u32[]{:S(2)}) collective-permute-start(f32[8]{0:T(128)S(1)} %add.249), channel_id=1, source_target_pairs={{0,16},{16,0},{32,48},{48,32},{64,80},{80,64},{96,112},{112,96},{1... | collective-permute-start | bytes 104 | tf_op jit(solution)/shard_map/ppermute | solution.py:27
  172.9 4.5 %collective-permute-start.21 = (f32[8]{0:T(128)S(1)}, f32[8]{0:T(128)S(1)}, u32[]{:S(2)}, u32[]{:S(2)}) collective-permute-start(f32[8]{0:T(128)S(1)} %add.250), channel_id=1, source_target_pairs={{0,32},{16,48},{32,0},{48,16},{64,96},{80,112},{96,64},{112,80},{1... | collective-permute-start | bytes 104 | tf_op jit(solution)/shard_map/ppermute | solution.py:27
  177.4 3.6 %collective-permute-start.22 = (f32[8]{0:T(128)S(1)}, f32[8]{0:T(128)S(1)}, u32[]{:S(2)}, u32[]{:S(2)}) collective-permute-start(f32[8]{0:T(128)S(1)} %add.251), channel_id=1, source_target_pairs={{0,64},{16,80},{32,96},{48,112},{64,0},{80,16},{96,32},{112,48},{1... | collective-permute-start | bytes 104 | tf_op jit(solution)/shard_map/ppermute | solution.py:27
  181.0 5.1 %collective-permute-start.23 = (f32[8]{0:T(128)S(1)}, f32[8]{0:T(128)S(1)}, u32[]{:S(2)}, u32[]{:S(2)}) collective-permute-start(f32[8]{0:T(128)S(1)} %add.252), channel_id=1, source_target_pairs={{0,128},{16,144},{32,160},{48,176},{64,192},{80,208},{96,224},{112... | collective-permute-start | bytes 104 | tf_op jit(solution)/shard_map/ppermute | solution.py:27
  189.1 1.4 collective-permute-start.24
  190.6 21.7 %collective-permute-start.25 = (f32[8,4097]{1,0:T(8,128)S(1)}, f32[8,4097]{1,0:T(8,128)S(1)}, u32[]{:S(2)}, u32[]{:S(2)}) collective-permute-start(f32[8,4097]{1,0:T(8,128)S(1)} %fusion.58), channel_id=1, source_target_pairs={{0,2},{1,3},{2,0},{3,1},{4,6},{5,7},{6,4},{7,5},{8,10},{9,11},{10,... | collective-permute-start | bytes 393320 | tf_op jit(solution)/shard_map/ppermute | solution.py:27
  212.3 5.6 %collective-permute-start.26 = (f32[8,4097]{1,0:T(8,128)S(1)}, f32[8,4097]{1,0:T(8,128)S(1)}, u32[]{:S(2)}, u32[]{:S(2)}) collective-permute-start(f32[8,4097]{1,0:T(8,128)S(1)} %add.255), channel_id=1, source_target_pairs={{0,4},{1,5},{2,6},{3,7},{4,0},{5,1},{6,2},{7,3},{8,12},{9,13},{10,... | collective-permute-start | bytes 393320 | tf_op jit(solution)/shard_map/ppermute | solution.py:27
  218.0 6.6 %collective-permute-start.27 = (f32[8,4097]{1,0:T(8,128)S(1)}, f32[8,4097]{1,0:T(8,128)S(1)}, u32[]{:S(2)}, u32[]{:S(2)}) collective-permute-start(f32[8,4097]{1,0:T(8,128)S(1)} %add.256), channel_id=1, source_target_pairs={{0,8},{1,9},{2,10},{3,11},{4,12},{5,13},{6,14},{7,15},{8,0},{9,1},... | collective-permute-start | bytes 393320 | tf_op jit(solution)/shard_map/ppermute | solution.py:27
  224.6 5.1 %collective-permute-start.28 = (f32[8,4097]{1,0:T(8,128)S(1)}, f32[8,4097]{1,0:T(8,128)S(1)}, u32[]{:S(2)}, u32[]{:S(2)}) collective-permute-start(f32[8,4097]{1,0:T(8,128)S(1)} %add.257), channel_id=1, source_target_pairs={{0,16},{16,0},{32,48},{48,32},{64,80},{80,64},{96,112},{112,96},{1... | collective-permute-start | bytes 393320 | tf_op jit(solution)/shard_map/ppermute | solution.py:27
  229.7 7.0 %collective-permute-start.29 = (f32[8,4097]{1,0:T(8,128)S(1)}, f32[8,4097]{1,0:T(8,128)S(1)}, u32[]{:S(2)}, u32[]{:S(2)}) collective-permute-start(f32[8,4097]{1,0:T(8,128)S(1)} %add.258), channel_id=1, source_target_pairs={{0,32},{16,48},{32,0},{48,16},{64,96},{80,112},{96,64},{112,80},{1... | collective-permute-start | bytes 393320 | tf_op jit(solution)/shard_map/ppermute | solution.py:27
  236.7 6.5 %collective-permute-start.30 = (f32[8,4097]{1,0:T(8,128)S(1)}, f32[8,4097]{1,0:T(8,128)S(1)}, u32[]{:S(2)}, u32[]{:S(2)}) collective-permute-start(f32[8,4097]{1,0:T(8,128)S(1)} %add.259), channel_id=1, source_target_pairs={{0,64},{16,80},{32,96},{48,112},{64,0},{80,16},{96,32},{112,48},{1... | collective-permute-start | bytes 393320 | tf_op jit(solution)/shard_map/ppermute | solution.py:27
  243.2 6.6 %collective-permute-start.31 = (f32[8,4097]{1,0:T(8,128)S(1)}, f32[8,4097]{1,0:T(8,128)S(1)}, u32[]{:S(2)}, u32[]{:S(2)}) collective-permute-start(f32[8,4097]{1,0:T(8,128)S(1)} %add.260), channel_id=1, source_target_pairs={{0,128},{16,144},{32,160},{48,176},{64,192},{80,208},{96,224},{112... | collective-permute-start | bytes 393320 | tf_op jit(solution)/shard_map/ppermute | solution.py:27
  250.8 5.9 %collective-permute-start.33 = (bf16[1,1,8,8,192]{4,3,2,1,0:T(8,128)(2,1)S(1)}, bf16[1,1,8,8,192]{4,3,2,1,0:T(8,128)(2,1)S(1)}, u32[]{:S(2)}, u32[]{:S(2)}) collective-permute-start(bf16[1,1,8,8,192]{4,3,2,1,0:T(8,128)(2,1)S(1)} %bitcast.156), channel_id=1, source_target_pairs={{16,0},{32,16},{48,32},{64,48},{80,64},{96,80},{112,96},{128,112},... | collective-permute-start | bytes 73736 | tf_op jit(solution)/shard_map/ppermute | solution.py:40
  252.7 8.5 %collective-permute-start.32 = (bf16[1,1,8,8,192]{4,3,2,1,0:T(8,128)(2,1)S(1)}, bf16[1,1,8,8,192]{4,3,2,1,0:T(8,128)(2,1)S(1)}, u32[]{:S(2)}, u32[]{:S(2)}) collective-permute-start(bf16[1,1,8,8,192]{4,3,2,1,0:T(8,128)(2,1)S(1)} %bitcast.157), channel_id=1, source_target_pairs={{0,16},{16,32},{32,48},{48,64},{64,80},{80,96},{96,112},{112,128},... | collective-permute-start | bytes 73736 | tf_op jit(solution)/shard_map/ppermute | solution.py:39
  261.2 4.3 %collective-permute-start.35 = (bf16[3,1,8,8,192]{4,3,2,1,0:T(8,128)(2,1)S(1)}, bf16[3,1,8,8,192]{4,3,2,1,0:T(8,128)(2,1)S(1)}, u32[]{:S(2)}, u32[]{:S(2)}) collective-permute-start(bf16[3,1,8,8,192]{4,3,2,1,0:T(8,128)(2,1)S(1)} %pad_maximum_fusion.9), channel_id=1, source_target_pairs={{1,0},{2,1},{3,2},{4,3},{5,4},{6,5},{7,6},{8,7},{9,8},{10,9},{11,1... | collective-permute-start | bytes 221192 | tf_op jit(solution)/shard_map/ppermute | solution.py:40
  263.2 10.7 %collective-permute-start.34 = (bf16[3,1,8,8,192]{4,3,2,1,0:T(8,128)(2,1)S(1)}, bf16[3,1,8,8,192]{4,3,2,1,0:T(8,128)(2,1)S(1)}, u32[]{:S(2)}, u32[]{:S(2)}) collective-permute-start(bf16[3,1,8,8,192]{4,3,2,1,0:T(8,128)(2,1)S(1)} %pad_maximum_fusion.9), channel_id=1, source_target_pairs={{0,1},{1,2},{2,3},{3,4},{4,5},{5,6},{6,7},{7,8},{8,9},{9,10},{10,1... | collective-permute-start | bytes 221192 | tf_op jit(solution)/shard_map/ppermute | solution.py:39
  281.1 6.9 %collective-permute-start.37 = (bf16[1,3,8,8,192]{4,3,2,1,0:T(8,128)(2,1)S(1)}, bf16[1,3,8,8,192]{4,3,2,1,0:T(8,128)(2,1)S(1)}, u32[]{:S(2)}, u32[]{:S(2)}) collective-permute-start(bf16[1,3,8,8,192]{4,3,2,1,0:T(8,128)(2,1)S(1)} %get-tuple-element.14), channel_id=1, source_target_pairs={{16,0},{32,16},{48,32},{64,48},{80,64},{96,80},{112,96},{128,112},... | collective-permute-start | bytes 221192 | tf_op jit(solution)/shard_map/ppermute | solution.py:40
  283.0 9.3 %collective-permute-start.36 = (bf16[1,3,8,8,192]{4,3,2,1,0:T(8,128)(2,1)S(1)}, bf16[1,3,8,8,192]{4,3,2,1,0:T(8,128)(2,1)S(1)}, u32[]{:S(2)}, u32[]{:S(2)}) collective-permute-start(bf16[1,3,8,8,192]{4,3,2,1,0:T(8,128)(2,1)S(1)} %get-tuple-element.13), channel_id=1, source_target_pairs={{0,16},{16,32},{32,48},{48,64},{64,80},{80,96},{96,112},{112,128},... | collective-permute-start | bytes 221192 | tf_op jit(solution)/shard_map/ppermute | solution.py:39
  292.4 4.7 %collective-permute-start.39 = (bf16[5,1,8,8,192]{4,3,2,1,0:T(8,128)(2,1)S(1)}, bf16[5,1,8,8,192]{4,3,2,1,0:T(8,128)(2,1)S(1)}, u32[]{:S(2)}, u32[]{:S(2)}) collective-permute-start(bf16[5,1,8,8,192]{4,3,2,1,0:T(8,128)(2,1)S(1)} %get-tuple-element.10), channel_id=1, source_target_pairs={{1,0},{2,1},{3,2},{4,3},{5,4},{6,5},{7,6},{8,7},{9,8},{10,9},{11,1... | collective-permute-start | bytes 368648 | tf_op jit(solution)/shard_map/ppermute | solution.py:40
  294.3 12.7 %collective-permute-start.38 = (bf16[5,1,8,8,192]{4,3,2,1,0:T(8,128)(2,1)S(1)}, bf16[5,1,8,8,192]{4,3,2,1,0:T(8,128)(2,1)S(1)}, u32[]{:S(2)}, u32[]{:S(2)}) collective-permute-start(bf16[5,1,8,8,192]{4,3,2,1,0:T(8,128)(2,1)S(1)} %get-tuple-element.9), channel_id=1, source_target_pairs={{0,1},{1,2},{2,3},{3,4},{4,5},{5,6},{6,7},{7,8},{8,9},{9,10},{10,1... | collective-permute-start | bytes 368648 | tf_op jit(solution)/shard_map/ppermute | solution.py:39
  313.8 1.2 collective-permute-start.40
  315.0 7.5 %collective-permute-start.41 = (f32[8]{0:T(128)S(1)}, f32[8]{0:T(128)S(1)}, u32[]{:S(2)}, u32[]{:S(2)}) collective-permute-start(f32[8]{0:T(128)S(1)} %add.277), channel_id=1, source_target_pairs={{0,2},{1,3},{2,0},{3,1},{4,6},{5,7},{6,4},{7,5},{8,10},{9,11},{10,... | collective-permute-start | bytes 104 | tf_op jit(solution)/shard_map/ppermute | solution.py:27
  322.5 3.6 %collective-permute-start.42 = (f32[8]{0:T(128)S(1)}, f32[8]{0:T(128)S(1)}, u32[]{:S(2)}, u32[]{:S(2)}) collective-permute-start(f32[8]{0:T(128)S(1)} %add.278), channel_id=1, source_target_pairs={{0,4},{1,5},{2,6},{3,7},{4,0},{5,1},{6,2},{7,3},{8,12},{9,13},{10,... | collective-permute-start | bytes 104 | tf_op jit(solution)/shard_map/ppermute | solution.py:27
  326.1 5.1 %collective-permute-start.43 = (f32[8]{0:T(128)S(1)}, f32[8]{0:T(128)S(1)}, u32[]{:S(2)}, u32[]{:S(2)}) collective-permute-start(f32[8]{0:T(128)S(1)} %add.279), channel_id=1, source_target_pairs={{0,8},{1,9},{2,10},{3,11},{4,12},{5,13},{6,14},{7,15},{8,0},{9,1},... | collective-permute-start | bytes 104 | tf_op jit(solution)/shard_map/ppermute | solution.py:27
  331.2 3.6 %collective-permute-start.44 = (f32[8]{0:T(128)S(1)}, f32[8]{0:T(128)S(1)}, u32[]{:S(2)}, u32[]{:S(2)}) collective-permute-start(f32[8]{0:T(128)S(1)} %add.280), channel_id=1, source_target_pairs={{0,16},{16,0},{32,48},{48,32},{64,80},{80,64},{96,112},{112,96},{1... | collective-permute-start | bytes 104 | tf_op jit(solution)/shard_map/ppermute | solution.py:27
  334.7 4.5 %collective-permute-start.45 = (f32[8]{0:T(128)S(1)}, f32[8]{0:T(128)S(1)}, u32[]{:S(2)}, u32[]{:S(2)}) collective-permute-start(f32[8]{0:T(128)S(1)} %add.281), channel_id=1, source_target_pairs={{0,32},{16,48},{32,0},{48,16},{64,96},{80,112},{96,64},{112,80},{1... | collective-permute-start | bytes 104 | tf_op jit(solution)/shard_map/ppermute | solution.py:27
  339.2 3.6 %collective-permute-start.46 = (f32[8]{0:T(128)S(1)}, f32[8]{0:T(128)S(1)}, u32[]{:S(2)}, u32[]{:S(2)}) collective-permute-start(f32[8]{0:T(128)S(1)} %add.282), channel_id=1, source_target_pairs={{0,64},{16,80},{32,96},{48,112},{64,0},{80,16},{96,32},{112,48},{1... | collective-permute-start | bytes 104 | tf_op jit(solution)/shard_map/ppermute | solution.py:27
  342.8 5.1 %collective-permute-start.47 = (f32[8]{0:T(128)S(1)}, f32[8]{0:T(128)S(1)}, u32[]{:S(2)}, u32[]{:S(2)}) collective-permute-start(f32[8]{0:T(128)S(1)} %add.283), channel_id=1, source_target_pairs={{0,128},{16,144},{32,160},{48,176},{64,192},{80,208},{96,224},{112... | collective-permute-start | bytes 104 | tf_op jit(solution)/shard_map/ppermute | solution.py:27
  (11 other events, 446.1 us)
where the time goes:
time: 353 us; the launch traced here: 349 us
  waiting for transfers between devices  181 us (51%)
  starting transfers between devices  86.4 us (24%)
  matrix products  45.5 us (13%)
  local copies, waits for them, and re-layouts  28.4 us (8%)
  other arithmetic  6.12 us (2%)
    ppermute x32, waiting for transfers between devices, all_sum(): x = x + lax.ppermute(x, axis, pairs)  126 us
    ppermute x8, waiting for transfers between devices, padded_2(): before = lax.ppermute(last, axis, up)  52.7 us
    ppermute x32, starting transfers between devices, all_sum(): x = x + lax.ppermute(x, axis, pairs)  45.4 us
    ppermute x8, starting transfers between devices, padded_2(): before = lax.ppermute(last, axis, up)  23.5 us
    ppermute x8, starting transfers between devices, padded_2(): after = lax.ppermute(initial, axis, down)  17.5 us
    another operation x1, local copies, waits for them, and re-layouts, masked_blocks(): stiffness.reshape(leading + (DOF, DOF)) * wide.astype(stiffness.dtype)  16.6 us
    dot_general x2, matrix products, per_device(): jnp.einsum('bsij,bslj->bli', weights, gathered, preferred_element_type=jn...  13.7 us
    dot_general x2, matrix products, per_device(): jnp.einsum('bsij,bli->bslj', weights, rounded, preferred_element_type=jnp...  11.6 us
  transfers between devices with their start and end apart: 48, of which 43 were waited for; matrix products, arithmetic and copies ran while one was open for 10% of the time, Pallas kernels for 0%

commit v1 on v0

--- a/solution.py
+++ b/solution.py
@@ -29,19 +29,6 @@
     return x
 
 
-def padded_2(x, sides, width):
-    for axis, dim in sides:
-        size, length = (lax.axis_size(axis), x.shape[dim])
-        up = [(i, (i + 1) % size) for i in range(size - 1)]
-        down = [(j, i) for i, j in up]
-        last = lax.slice_in_dim(x, length - width, length, axis=dim)
-        initial = lax.slice_in_dim(x, 0, width, axis=dim)
-        before = lax.ppermute(last, axis, up)
-        after = lax.ppermute(initial, axis, down)
-        x = jnp.concatenate([before, x, after], axis=dim)
-    return x
-
-
 def unpack_bits(packed):
     shifts = jnp.arange(16, dtype=jnp.int32)
     bitset = jnp.right_shift(packed[..., None], shifts) & 1
@@ -58,6 +45,21 @@
     return stiffness.reshape(leading + (DOF, DOF)) * wide.astype(stiffness.dtype)
 
 
+def neighbour_swap(parts, mesh_shape):
+    nx, ny = mesh_shape
+    arrived = {}
+    for (a, c), value in parts.items():
+        dx, dy = a - 1, c - 1
+        pairs = [
+            (i * ny + j, (i + dx) * ny + (j + dy))
+            for i in range(nx)
+            for j in range(ny)
+            if 0 <= i + dx < nx and 0 <= j + dy < ny
+        ]
+        arrived[(2 - a, 2 - c)] = lax.ppermute(value, ("gx", "gy"), pairs)
+    return arrived
+
+
 def per_device(
     load_vectors,
     bond_stiffness,
@@ -68,6 +70,8 @@
     coarse_basis,
     coarse_factor,
 ):
+    mesh_shape = (lax.axis_size("gx"), lax.axis_size("gy"))
+    sides = [(a, c) for a in range(3) for c in range(3) if (a, c) != (1, 1)]
     weights = masked_blocks(bond_stiffness[0, 0], intact_words[0, 0])
     row_total = jnp.sum(weights, axis=(1, 3), dtype=jnp.float32)
     column_total = jnp.sum(weights, axis=2, dtype=jnp.float32)
@@ -80,6 +84,20 @@
     self_block = self_stiffness[0, 0].reshape(BZ, DOF, DOF)
     inverse = block_inverse[0, 0].reshape(BZ, DOF, DOF)
     coarse_vecs = coarse_basis[0, 0]
+
+    def spread_terms(flat_terms, tail):
+        high_part = flat_terms.astype(jnp.bfloat16)
+        low_part = (flat_terms - high_part.astype(jnp.float32)).astype(jnp.bfloat16)
+        spread = jnp.dot(selector, high_part, preferred_element_type=jnp.float32) + jnp.dot(
+            selector, low_part, preferred_element_type=jnp.float32
+        )
+        return spread.reshape((3, 3, depth_span) + tail)[:, :, 1 : depth_span - 1]
+
+    column_spread = spread_terms(column_total.reshape(BZ * NS, DOF), (DOF,))
+    column_in = neighbour_swap({side: column_spread[side] for side in sides}, mesh_shape)
+    column_fold = column_spread[1, 1]
+    for side in sides:
+        column_fold = column_fold + column_in[side]
 
     def precondition(residual):
         own_part = jnp.einsum("bij,blj->bli", inverse, residual, precision=highest)
@@ -99,7 +117,17 @@
     direction = smoothed
     for iteration in range(ITERS):
         rounded = direction.astype(jnp.bfloat16)
-        ghosts = padded_2(rounded[None, None], (("gx", 0), ("gy", 1)), 1)
+        backward = -jnp.einsum("bsij,bli->bslj", weights, rounded, preferred_element_type=jnp.float32)
+        partial_value = spread_terms(backward.reshape(BZ * NS, NLOAD * DOF), (NLOAD, DOF))
+        high = partial_value.astype(jnp.bfloat16)
+        low = (partial_value - high.astype(jnp.float32)).astype(jnp.bfloat16)
+        outgoing = {side: jnp.stack([rounded, high[side], low[side]]) for side in sides}
+        arrived = neighbour_swap(outgoing, mesh_shape)
+        ghost_rows = []
+        for a in range(3):
+            for c in range(3):
+                ghost_rows.append(rounded if (a, c) == (1, 1) else arrived[(a, c)][0])
+        ghosts = jnp.stack(ghost_rows).reshape(3, 3, BZ, NLOAD, DOF)
         padded = jnp.pad(ghosts, ((0, 0), (0, 0), (1, 1), (0, 0), (0, 0))).reshape(
             ghost_count, NLOAD, DOF
         )
@@ -107,27 +135,11 @@
         forward = row_total[:, None, :] * rounded - jnp.einsum(
             "bsij,bslj->bli", weights, gathered, preferred_element_type=jnp.float32
         )
-        backward = column_total[:, :, None, :] * gathered - jnp.einsum(
-            "bsij,bli->bslj", weights, rounded, preferred_element_type=jnp.float32
-        )
-        flat_terms = backward.reshape(BZ * NS, NLOAD * DOF)
-        high_part = flat_terms.astype(jnp.bfloat16)
-        low_part = (flat_terms - high_part.astype(jnp.float32)).astype(jnp.bfloat16)
-        apply_spread = jnp.dot(selector, high_part, preferred_element_type=jnp.float32) + jnp.dot(
-            selector, low_part, preferred_element_type=jnp.float32
-        )
-        partial_value = apply_spread.reshape(3, 3, depth_span, NLOAD, DOF)[:, :, 1 : depth_span - 1]
-        beside_all = padded_2(partial_value.astype(jnp.bfloat16), (("gx", 0), ("gy", 1)), 1).astype(
-            partial_value.dtype
-        )
-        folded = (
-            beside_all[2, 2]
-            + beside_all[0, 0]
-            + beside_all[0, 2]
-            + beside_all[0, 4]
-            + beside_all[2, 0]
-        )
-        folded = folded + beside_all[2, 4] + beside_all[4, 0] + beside_all[4, 2] + beside_all[4, 4]
+        folded = partial_value[1, 1]
+        for side in sides:
+            got = arrived[side]
+            folded = folded + (got[1].astype(jnp.float32) + got[2].astype(jnp.float32))
+        folded = folded + column_fold[:, None, :] * rounded.astype(jnp.float32)
         diagonal = jnp.einsum(
             "bij,blj->bli", self_block, rounded, preferred_element_type=jnp.float32
         )

time: 353 us -> 371 us (1.051)
  starting transfers between devices: 86.4 us -> 164 us
  waiting for transfers between devices: 181 us -> 115 us
  matrix products: 45.5 us -> 49.6 us
    ppermute x16 -> x24, starting transfers between devices: 41.1 us -> 104 us  [neighbour_swap(): arrived[2 - a, 2 - c] = lax.ppermute(value, ('gx', 'gy'), pairs)]
    ppermute x16 -> x24, waiting for transfers between devices: 55.1 us -> 4.17 us  [neighbour_swap(): arrived[2 - a, 2 - c] = lax.ppermute(value, ('gx', 'gy'), pairs)]
    ppermute x32, waiting for transfers between devices: 126 us -> 110 us  [all_sum(): x = x + lax.ppermute(x, axis, pairs)]
    ppermute x32, starting transfers between devices: 45.4 us -> 60.2 us  [all_sum(): x = x + lax.ppermute(x, axis, pairs)]
  transfers between devices with their start and end apart: 48 -> 56, of which waited for: 43 -> 30; matrix products, arithmetic and copies ran while one was open for 10% -> 10% of each run, Pallas kernels for 0% -> 0%
where the time goes in v1:
time: 371 us; the launch traced here: 365 us
  starting transfers between devices  164 us (44%)
  waiting for transfers between devices  115 us (31%)
  matrix products  49.6 us (13%)
  local copies, waits for them, and re-layouts  29.4 us (8%)
  other arithmetic  5.57 us (2%)
    ppermute x32, waiting for transfers between devices, all_sum(): x = x + lax.ppermute(x, axis, pairs)  110 us
    ppermute x24, starting transfers between devices, neighbour_swap(): arrived[2 - a, 2 - c] = lax.ppermute(value, ('gx', 'gy'), pairs)  104 us
    ppermute x32, starting transfers between devices, all_sum(): x = x + lax.ppermute(x, axis, pairs)  60.2 us
    another operation x1, local copies, waits for them, and re-layouts, masked_blocks(): stiffness.reshape(leading + (DOF, DOF)) * wide.astype(stiffness.dtype)  16.6 us
    dot_general x2, matrix products, per_device(): jnp.einsum('bsij,bslj->bli', weights, gathered, preferred_element_type=jn...  13.8 us
    dot_general x2, matrix products, per_device(): jnp.einsum('bsij,bli->bslj', weights, rounded, preferred_element_type=jnp...  11.6 us
    dot_general x1, matrix products, masked_blocks(): jnp.einsum('Ii,...ij,Jj->...IJ', spread, intact, spread, preferred_elemen...  10.8 us
  transfers between devices with their start and end apart: 56, of which 30 were waited for; matrix products, arithmetic and copies ran while one was open for 10% of the time, Pallas kernels for 0%

profile of v1, /device:TPU:14, one launch (start us, length us, event | category | flops | bytes accessed | tf_op | source)
XLA Modules:
  0.0 364.8 jit_solution(10191504656159278661)
XLA Ops:
  3.9 3.1 fusion.70
  7.4 16.6 %reshape_squeeze.11 = bf16[8,13,192,192]{3,2,0,1:T(8,128)(2,1)} reshape(bf16[1,1,8,13,36864]{4,2,3,1,0:T(8,128)(2,1)} %param.11) | data formatting | bytes 15335424 | tf_op jit(solution)/shard_map/reshape;squeeze | solution.py:45
  26.1 7.3 %collective-permute-start.1 = (f32[8,4097]{1,0:T(8,128)S(1)}, f32[8,4097]{1,0:T(8,128)S(1)}, u32[]{:S(2)}, u32[]{:S(2)}) collective-permute-start(f32[8,4097]{1,0:T(8,128)S(1)} %fusion.102), channel_id=1, source_target_pairs={{0,2},{1,3},{2,0},{3,1},{4,6},{5,7},{6,4},{7,5},{8,10},{9,11},{10,... | collective-permute-start | bytes 393320 | tf_op jit(solution)/shard_map/ppermute | solution.py:27
  33.3 10.8 %convert_reduce_fusion.1 = (f32[8,192]{1,0:T(8,128)S(1)}, f32[8,13,192]{2,1,0:T(8,128)S(1)}, bf16[8,13,192,192]{3,2,1,0:T(8,128)(2,1)}) fusion(s32[192]{0:T(256)S(1)} %and_select_fusion, bf16[8,13,64,64]{2,3,1,0:T(8,128)(2,1)} %fusion.1, bf16[8,13,192,192]{3,2,0,1:T(8,128)(2,1)} %reshape_squeeze.11), kind=kOutput, calls=%fused_computation.3 | convolution fusion | flops 684985344 | bytes 16274176 | tf_op jit(solution)/shard_map/Ii,...ij,Jj->...IJ/dot_general | solution.py:44
  45.3 4.7 %collective-permute-done.2 = f32[8,4097]{1,0:T(8,128)S(1)} collective-permute-done((f32[8,4097]{1,0:T(8,128)S(1)}, f32[8,4097]{1,0:T(8,128)S(1)}, u32[]{:S(2)}, u32[]{:S(2)}) %collective-permute-start.2) | collective-permute-done | bytes 131136 | tf_op jit(solution)/shard_map/ppermute | solution.py:27
  51.8 4.9 %collective-permute-done.3 = f32[8,4097]{1,0:T(8,128)S(1)} collective-permute-done((f32[8,4097]{1,0:T(8,128)S(1)}, f32[8,4097]{1,0:T(8,128)S(1)}, u32[]{:S(2)}, u32[]{:S(2)}) %collective-permute-start.3) | collective-permute-done | bytes 131136 | tf_op jit(solution)/shard_map/ppermute | solution.py:27
  63.3 7.3 %collective-permute-start.18 = (f32[8,192]{1,0:T(8,128)S(1)}, f32[8,192]{1,0:T(8,128)S(1)}, u32[]{:S(2)}, u32[]{:S(2)}) collective-permute-start(f32[8,192]{1,0:T(8,128)S(1)} %get-tuple-element.51), channel_id=1, source_target_pairs={{1,16},{2,17},{3,18},{4,19},{5,20},{6,21},{7,22},{8,23},{9,24},{10... | collective-permute-start | bytes 18440 | tf_op jit(solution)/shard_map/ppermute | solution.py:59
  72.5 3.4 collective-permute-start.5
  76.0 6.3 %collective-permute-done.5 = f32[8,4097]{1,0:T(8,128)S(1)} collective-permute-done((f32[8,4097]{1,0:T(8,128)S(1)}, f32[8,4097]{1,0:T(8,128)S(1)}, u32[]{:S(2)}, u32[]{:S(2)}) %collective-permute-start.5) | collective-permute-done | bytes 131136 | tf_op jit(solution)/shard_map/ppermute | solution.py:27
  82.9 5.2 %collective-permute-start.20 = (f32[8,192]{1,0:T(8,128)}, f32[8,192]{1,0:T(8,128)S(1)}, u32[]{:S(2)}, u32[]{:S(2)}) collective-permute-start(f32[8,192]{1,0:T(8,128)} %get-tuple-element.49), channel_id=1, source_target_pairs={{1,0},{2,1},{3,2},{4,3},{5,4},{6,5},{7,6},{8,7},{9,8},{10,9},{11,1... | collective-permute-start | bytes 18440 | tf_op jit(solution)/shard_map/ppermute | solution.py:59
  90.2 3.0 collective-permute-start.22
  93.2 6.4 %collective-permute-start.23 = (f32[8,192]{1,0:T(8,128)S(1)}, f32[8,192]{1,0:T(8,128)}, u32[]{:S(2)}, u32[]{:S(2)}) collective-permute-start(f32[8,192]{1,0:T(8,128)S(1)} %get-tuple-element.46), channel_id=1, source_target_pairs={{17,0},{18,1},{19,2},{20,3},{21,4},{22,5},{23,6},{24,7},{25,8},{26... | collective-permute-start | bytes 18440 | tf_op jit(solution)/shard_map/ppermute | solution.py:59
  103.8 4.6 %collective-permute-done.7 = f32[8,4097]{1,0:T(8,128)S(1)} collective-permute-done((f32[8,4097]{1,0:T(8,128)S(1)}, f32[8,4097]{1,0:T(8,128)S(1)}, u32[]{:S(2)}, u32[]{:S(2)}) %collective-permute-start.7) | collective-permute-done | bytes 131136 | tf_op jit(solution)/shard_map/ppermute | solution.py:27
  110.7 6.2 %fusion.5 = f32[8,13,8,192]{3,2,1,0:T(8,128)} fusion(bf16[8,13,192,192]{3,2,1,0:T(8,128)(2,1)} %get-tuple-element.75, bf16[8,8,192]{2,1,0:T(8,128)(2,1)S(1)} %get-tuple-element.73), kind=kOutput, calls=%fused_computation.14 | convolution fusion | flops 61501440 | bytes 8331264 | tf_op jit(solution)/shard_map/bsij,bli->bslj/dot_general | solution.py:120
  123.1 5.4 %collective-permute-start.9 = (bf16[3,8,8,192]{3,2,1,0:T(8,128)(2,1)S(1)}, bf16[3,8,8,192]{3,2,1,0:T(8,128)(2,1)S(1)}, u32[]{:S(2)}, u32[]{:S(2)}) collective-permute-start(bf16[3,8,8,192]{3,2,1,0:T(8,128)(2,1)S(1)} %get-tuple-element.67), channel_id=1, source_target_pairs={{0,16},{1,17},{2,18},{3,19},{4,20},{5,21},{6,22},{7,23},{8,24},{9,... | collective-permute-start | bytes 221192 | tf_op jit(solution)/shard_map/ppermute | solution.py:59
  128.6 5.5 %collective-permute-start.10 = (bf16[3,8,8,192]{3,2,1,0:T(8,128)(2,1)S(1)}, bf16[3,8,8,192]{3,2,1,0:T(8,128)(2,1)S(1)}, u32[]{:S(2)}, u32[]{:S(2)}) collective-permute-start(bf16[3,8,8,192]{3,2,1,0:T(8,128)(2,1)S(1)} %get-tuple-element.62), channel_id=1, source_target_pairs={{1,16},{2,17},{3,18},{4,19},{5,20},{6,21},{7,22},{8,23},{9,24},{10... | collective-permute-start | bytes 221192 | tf_op jit(solution)/shard_map/ppermute | solution.py:59
  136.0 8.4 %collective-permute-start.12 = (bf16[3,8,8,192]{3,2,1,0:T(8,128)(2,1)S(1)}, bf16[3,8,8,192]{3,2,1,0:T(8,128)(2,1)S(1)}, u32[]{:S(2)}, u32[]{:S(2)}) collective-permute-start(bf16[3,8,8,192]{3,2,1,0:T(8,128)(2,1)S(1)} %get-tuple-element.64), channel_id=1, source_target_pairs={{1,0},{2,1},{3,2},{4,3},{5,4},{6,5},{7,6},{8,7},{9,8},{10,9},{11,1... | collective-permute-start | bytes 221192 | tf_op jit(solution)/shard_map/ppermute | solution.py:59
  148.7 4.9 %collective-permute-start.14 = (bf16[3,8,8,192]{3,2,1,0:T(8,128)(2,1)S(1)}, bf16[3,8,8,192]{3,2,1,0:T(8,128)(2,1)S(1)}, u32[]{:S(2)}, u32[]{:S(2)}) collective-permute-start(bf16[3,8,8,192]{3,2,1,0:T(8,128)(2,1)S(1)} %get-tuple-element.66), channel_id=1, source_target_pairs={{16,0},{17,1},{18,2},{19,3},{20,4},{21,5},{22,6},{23,7},{24,8},{25... | collective-permute-start | bytes 221192 | tf_op jit(solution)/shard_map/ppermute | solution.py:59
  153.7 7.3 %collective-permute-start.15 = (bf16[3,8,8,192]{3,2,1,0:T(8,128)(2,1)S(1)}, bf16[3,8,8,192]{3,2,1,0:T(8,128)(2,1)S(1)}, u32[]{:S(2)}, u32[]{:S(2)}) collective-permute-start(bf16[3,8,8,192]{3,2,1,0:T(8,128)(2,1)S(1)} %get-tuple-element.68), channel_id=1, source_target_pairs={{17,0},{18,1},{19,2},{20,3},{21,4},{22,5},{23,6},{24,7},{25,8},{26... | collective-permute-start | bytes 221192 | tf_op jit(solution)/shard_map/ppermute | solution.py:59
  166.4 7.0 %multiply_reduce_fusion.4 = (f32[8]{0:T(128)S(1)}, f32[8,8,192]{2,1,0:T(8,128)S(1)}) fusion(f32[8,8,192]{2,1,0:T(8,128)} %get-tuple-element.74, f32[8,192]{1,0:T(8,128)S(1)} %fusion.98, bf16[3,8,8,192]{3,2,1,0:T(8,128)(2,1)} %copy-done.16, bf16[3,8,8,192]{3,2,1,0:T(8,128)(2,1)} %copy-done.15, bf16[3,8,8,192]{3,2,1,0:T(8,128)(2,1)} %copy-done.14, ...), kind=kOutput, calls=%fused_computation.128 | convolution fusion | flops 62005240 | bytes 8614024 | tf_op jit(solution)/shard_map/bsij,bslj->bli/dot_general | solution.py:135
  174.7 7.5 %collective-permute-done.25 = f32[8]{0:T(128)S(1)} collective-permute-done((f32[8]{0:T(128)S(1)}, f32[8]{0:T(128)S(1)}, u32[]{:S(2)}, u32[]{:S(2)}) %collective-permute-start.25) | collective-permute-done | bytes 64 | tf_op jit(solution)/shard_map/ppermute | solution.py:27
  182.2 3.4 collective-permute-start.26
  196.1 4.3 %collective-permute-done.29 = f32[8]{0:T(128)S(1)} collective-permute-done((f32[8]{0:T(128)S(1)}, f32[8]{0:T(128)S(1)}, u32[]{:S(2)}, u32[]{:S(2)}) %collective-permute-start.29) | collective-permute-done | bytes 64 | tf_op jit(solution)/shard_map/ppermute | solution.py:27
  200.4 3.6 collective-permute-done.30
  204.9 4.1 %collective-permute-done.31 = f32[8]{0:T(128)S(1)} collective-permute-done((f32[8]{0:T(128)S(1)}, f32[8]{0:T(128)S(1)}, u32[]{:S(2)}, u32[]{:S(2)}) %collective-permute-start.31) | collective-permute-done | bytes 64 | tf_op jit(solution)/shard_map/ppermute | solution.py:27
  211.3 9.9 %collective-permute-start.32 = (f32[8,4097]{1,0:T(8,128)S(1)}, f32[8,4097]{1,0:T(8,128)S(1)}, u32[]{:S(2)}, u32[]{:S(2)}) collective-permute-start(f32[8,4097]{1,0:T(8,128)S(1)} %pad_maximum_fusion.17), channel_id=1, source_target_pairs={{0,1},{1,0},{2,3},{3,2},{4,5},{5,4},{6,7},{7,6},{8,9},{9,8},{10,11... | collective-permute-start | bytes 393320 | tf_op jit(solution)/shard_map/ppermute | solution.py:27
  222.5 5.9 %collective-permute-start.33 = (f32[8,4097]{1,0:T(8,128)S(1)}, f32[8,4097]{1,0:T(8,128)S(1)}, u32[]{:S(2)}, u32[]{:S(2)}) collective-permute-start(f32[8,4097]{1,0:T(8,128)S(1)} %fusion.101), channel_id=1, source_target_pairs={{0,2},{1,3},{2,0},{3,1},{4,6},{5,7},{6,4},{7,5},{8,10},{9,11},{10,... | collective-permute-start | bytes 393320 | tf_op jit(solution)/shard_map/ppermute | solution.py:27
  228.4 6.4 %collective-permute-done.33 = f32[8,4097]{1,0:T(8,128)S(1)} collective-permute-done((f32[8,4097]{1,0:T(8,128)S(1)}, f32[8,4097]{1,0:T(8,128)S(1)}, u32[]{:S(2)}, u32[]{:S(2)}) %collective-permute-start.33) | collective-permute-done | bytes 131136 | tf_op jit(solution)/shard_map/ppermute | solution.py:27
  236.9 3.6 collective-permute-done.34
  243.0 4.1 %collective-permute-done.35 = f32[8,4097]{1,0:T(8,128)S(1)} collective-permute-done((f32[8,4097]{1,0:T(8,128)S(1)}, f32[8,4097]{1,0:T(8,128)S(1)}, u32[]{:S(2)}, u32[]{:S(2)}) %collective-permute-start.35) | collective-permute-done | bytes 131136 | tf_op jit(solution)/shard_map/ppermute | solution.py:27
  248.8 3.6 collective-permute-done.36
  253.3 5.1 %collective-permute-done.37 = f32[8,4097]{1,0:T(8,128)S(1)} collective-permute-done((f32[8,4097]{1,0:T(8,128)S(1)}, f32[8,4097]{1,0:T(8,128)S(1)}, u32[]{:S(2)}, u32[]{:S(2)}) %collective-permute-start.37) | collective-permute-done | bytes 131136 | tf_op jit(solution)/shard_map/ppermute | solution.py:27
  258.9 5.5 %collective-permute-done.38 = f32[8,4097]{1,0:T(8,128)S(1)} collective-permute-done((f32[8,4097]{1,0:T(8,128)S(1)}, f32[8,4097]{1,0:T(8,128)S(1)}, u32[]{:S(2)}, u32[]{:S(2)}) %collective-permute-start.38) | collective-permute-done | bytes 131136 | tf_op jit(solution)/shard_map/ppermute | solution.py:27
  265.9 5.0 %collective-permute-done.39 = f32[8,4097]{1,0:T(8,128)S(1)} collective-permute-done((f32[8,4097]{1,0:T(8,128)S(1)}, f32[8,4097]{1,0:T(8,128)S(1)}, u32[]{:S(2)}, u32[]{:S(2)}) %collective-permute-start.39) | collective-permute-done | bytes 131136 | tf_op jit(solution)/shard_map/ppermute | solution.py:27
  272.8 5.3 %fusion.4 = f32[8,13,8,192]{3,2,1,0:T(8,128)S(1)} fusion(bf16[8,13,192,192]{3,2,1,0:T(8,128)(2,1)} %get-tuple-element.75, bf16[8,8,192]{2,1,0:T(8,128)(2,1)S(1)} %get-tuple-element.80), kind=kOutput, calls=%fused_computation.12 | convolution fusion | flops 61501440 | bytes 8331264 | tf_op jit(solution)/shard_map/bsij,bli->bslj/dot_general | solution.py:120
  281.6 3.8 %collective-permute-start.41 = (bf16[3,8,8,192]{3,2,1,0:T(8,128)(2,1)S(1)}, bf16[3,8,8,192]{3,2,1,0:T(8,128)(2,1)S(1)}, u32[]{:S(2)}, u32[]{:S(2)}) collective-permute-start(bf16[3,8,8,192]{3,2,1,0:T(8,128)(2,1)S(1)} %get-tuple-element.59), channel_id=1, source_target_pairs={{0,16},{1,17},{2,18},{3,19},{4,20},{5,21},{6,22},{7,23},{8,24},{9,... | collective-permute-start | bytes 221192 | tf_op jit(solution)/shard_map/ppermute | solution.py:59
  285.5 7.2 %collective-permute-start.42 = (bf16[3,8,8,192]{3,2,1,0:T(8,128)(2,1)S(1)}, bf16[3,8,8,192]{3,2,1,0:T(8,128)(2,1)S(1)}, u32[]{:S(2)}, u32[]{:S(2)}) collective-permute-start(bf16[3,8,8,192]{3,2,1,0:T(8,128)(2,1)S(1)} %get-tuple-element.54), channel_id=1, source_target_pairs={{1,16},{2,17},{3,18},{4,19},{5,20},{6,21},{7,22},{8,23},{9,24},{10... | collective-permute-start | bytes 221192 | tf_op jit(solution)/shard_map/ppermute | solution.py:59
  294.6 8.4 %collective-permute-start.44 = (bf16[3,8,8,192]{3,2,1,0:T(8,128)(2,1)S(1)}, bf16[3,8,8,192]{3,2,1,0:T(8,128)(2,1)S(1)}, u32[]{:S(2)}, u32[]{:S(2)}) collective-permute-start(bf16[3,8,8,192]{3,2,1,0:T(8,128)(2,1)S(1)} %get-tuple-element.56), channel_id=1, source_target_pairs={{1,0},{2,1},{3,2},{4,3},{5,4},{6,5},{7,6},{8,7},{9,8},{10,9},{11,1... | collective-permute-start | bytes 221192 | tf_op jit(solution)/shard_map/ppermute | solution.py:59
  305.0 3.3 collective-permute-start.46
  308.4 7.1 %collective-permute-start.47 = (bf16[3,8,8,192]{3,2,1,0:T(8,128)(2,1)S(1)}, bf16[3,8,8,192]{3,2,1,0:T(8,128)(2,1)S(1)}, u32[]{:S(2)}, u32[]{:S(2)}) collective-permute-start(bf16[3,8,8,192]{3,2,1,0:T(8,128)(2,1)S(1)} %get-tuple-element.60), channel_id=1, source_target_pairs={{17,0},{18,1},{19,2},{20,3},{21,4},{22,5},{23,6},{24,7},{25,8},{26... | collective-permute-start | bytes 221192 | tf_op jit(solution)/shard_map/ppermute | solution.py:59
  318.4 6.8 %multiply_reduce_fusion.2 = (f32[8]{0:T(128)S(1)}, f32[8,8,192]{2,1,0:T(8,128)S(1)}) fusion(f32[8,8,192]{2,1,0:T(8,128)S(1)} %get-tuple-element.81, f32[8,192]{1,0:T(8,128)S(1)} %fusion.98, bf16[3,8,8,192]{3,2,1,0:T(8,128)(2,1)S(1)} %collective-permute-done.47, bf16[3,8,8,192]{3,2,1,0:T(8,128)(2,1)S(1)} %collective-permute-done.46, ...), kind=kOutput, calls=%fused_computation.126 | convolution fusion | flops 62005240 | bytes 8614024 | tf_op jit(solution)/shard_map/bsij,bslj->bli/dot_general | solution.py:135
  325.2 5.0 %collective-permute-start.48 = (f32[8]{0:T(128)S(1)}, f32[8]{0:T(128)S(1)}, u32[]{:S(2)}, u32[]{:S(2)}) collective-permute-start(f32[8]{0:T(128)S(1)} %get-tuple-element.82), channel_id=1, source_target_pairs={{0,1},{1,0},{2,3},{3,2},{4,5},{5,4},{6,7},{7,6},{8,9},{9,8},{10,11... | collective-permute-start | bytes 104 | tf_op jit(solution)/shard_map/ppermute | solution.py:27
  331.1 7.5 %collective-permute-done.49 = f32[8]{0:T(128)S(1)} collective-permute-done((f32[8]{0:T(128)S(1)}, f32[8]{0:T(128)S(1)}, u32[]{:S(2)}, u32[]{:S(2)}) %collective-permute-start.49) | collective-permute-done | bytes 64 | tf_op jit(solution)/shard_map/ppermute | solution.py:27
  343.8 3.4 collective-permute-done.51
  347.2 3.6 collective-permute-done.52
  350.8 4.5 %collective-permute-done.53 = f32[8]{0:T(128)S(1)} collective-permute-done((f32[8]{0:T(128)S(1)}, f32[8]{0:T(128)S(1)}, u32[]{:S(2)}, u32[]{:S(2)}) %collective-permute-start.53) | collective-permute-done | bytes 64 | tf_op jit(solution)/shard_map/ppermute | solution.py:27
  355.3 3.6 collective-permute-done.54
  359.5 4.4 %collective-permute-done.55 = f32[8]{0:T(128)S(1)} collective-permute-done((f32[8]{0:T(128)S(1)}, f32[8]{0:T(128)S(1)}, u32[]{:S(2)}, u32[]{:S(2)}) %collective-permute-start.55) | collective-permute-done | bytes 64 | tf_op jit(solution)/shard_map/ppermute | solution.py:27
  (221 shorter events, 88.7 us)
Async XLA Ops:
  7.3 18.7 %collective-permute-start = (f32[8,4097]{1,0:T(8,128)S(1)}, f32[8,4097]{1,0:T(8,128)S(1)}, u32[]{:S(2)}, u32[]{:S(2)}) collective-permute-start(f32[8,4097]{1,0:T(8,128)S(1)} %pad_maximum_fusion.16), channel_id=1, source_target_pairs={{0,1},{1,0},{2,3},{3,2},{4,5},{5,4},{6,7},{7,6},{8,9},{9,8},{10,11... | collective-permute-start | bytes 393320 | tf_op jit(solution)/shard_map/ppermute | solution.py:27
  26.1 18.2 %collective-permute-start.1 = (f32[8,4097]{1,0:T(8,128)S(1)}, f32[8,4097]{1,0:T(8,128)S(1)}, u32[]{:S(2)}, u32[]{:S(2)}) collective-permute-start(f32[8,4097]{1,0:T(8,128)S(1)} %fusion.102), channel_id=1, source_target_pairs={{0,2},{1,3},{2,0},{3,1},{4,6},{5,7},{6,4},{7,5},{8,10},{9,11},{10,... | collective-permute-start | bytes 393320 | tf_op jit(solution)/shard_map/ppermute | solution.py:27
  44.3 5.8 %collective-permute-start.2 = (f32[8,4097]{1,0:T(8,128)S(1)}, f32[8,4097]{1,0:T(8,128)S(1)}, u32[]{:S(2)}, u32[]{:S(2)}) collective-permute-start(f32[8,4097]{1,0:T(8,128)S(1)} %add.341), channel_id=1, source_target_pairs={{0,4},{1,5},{2,6},{3,7},{4,0},{5,1},{6,2},{7,3},{8,12},{9,13},{10,... | collective-permute-start | bytes 393320 | tf_op jit(solution)/shard_map/ppermute | solution.py:27
  50.1 6.6 %collective-permute-start.3 = (f32[8,4097]{1,0:T(8,128)S(1)}, f32[8,4097]{1,0:T(8,128)S(1)}, u32[]{:S(2)}, u32[]{:S(2)}) collective-permute-start(f32[8,4097]{1,0:T(8,128)S(1)} %add.342), channel_id=1, source_target_pairs={{0,8},{1,9},{2,10},{3,11},{4,12},{5,13},{6,14},{7,15},{8,0},{9,1},... | collective-permute-start | bytes 393320 | tf_op jit(solution)/shard_map/ppermute | solution.py:27
  56.7 15.8 %collective-permute-start.4 = (f32[8,4097]{1,0:T(8,128)S(1)}, f32[8,4097]{1,0:T(8,128)S(1)}, u32[]{:S(2)}, u32[]{:S(2)}) collective-permute-start(f32[8,4097]{1,0:T(8,128)S(1)} %add.343), channel_id=1, source_target_pairs={{0,16},{16,0},{32,48},{48,32},{64,80},{80,64},{96,112},{112,96},{1... | collective-permute-start | bytes 393320 | tf_op jit(solution)/shard_map/ppermute | solution.py:27
  58.4 24.5 %collective-permute-start.16 = (f32[8,192]{1,0:T(8,128)S(1)}, f32[8,192]{1,0:T(8,128)S(1)}, u32[]{:S(2)}, u32[]{:S(2)}) collective-permute-start(f32[8,192]{1,0:T(8,128)S(1)} %get-tuple-element.45), channel_id=1, source_target_pairs={{0,17},{1,18},{2,19},{3,20},{4,21},{5,22},{6,23},{7,24},{8,25},{9,... | collective-permute-start | bytes 18440 | tf_op jit(solution)/shard_map/ppermute | solution.py:59
  60.3 27.9 %collective-permute-start.17 = (f32[8,192]{1,0:T(8,128)S(1)}, f32[8,192]{1,0:T(8,128)S(1)}, u32[]{:S(2)}, u32[]{:S(2)}) collective-permute-start(f32[8,192]{1,0:T(8,128)S(1)} %get-tuple-element.52), channel_id=1, source_target_pairs={{0,16},{1,17},{2,18},{3,19},{4,20},{5,21},{6,22},{7,23},{8,24},{9,... | collective-permute-start | bytes 18440 | tf_op jit(solution)/shard_map/ppermute | solution.py:59
  63.3 26.9 %collective-permute-start.18 = (f32[8,192]{1,0:T(8,128)S(1)}, f32[8,192]{1,0:T(8,128)S(1)}, u32[]{:S(2)}, u32[]{:S(2)}) collective-permute-start(f32[8,192]{1,0:T(8,128)S(1)} %get-tuple-element.51), channel_id=1, source_target_pairs={{1,16},{2,17},{3,18},{4,19},{5,20},{6,21},{7,22},{8,23},{9,24},{10... | collective-permute-start | bytes 18440 | tf_op jit(solution)/shard_map/ppermute | solution.py:59
  70.5 31.0 %collective-permute-start.19 = (f32[8,192]{1,0:T(8,128)}, f32[8,192]{1,0:T(8,128)}, u32[]{:S(2)}, u32[]{:S(2)}) collective-permute-start(f32[8,192]{1,0:T(8,128)} %get-tuple-element.50), channel_id=1, source_target_pairs={{0,1},{1,2},{2,3},{3,4},{4,5},{5,6},{6,7},{7,8},{8,9},{9,10},{10,1... | collective-permute-start | bytes 18440 | tf_op jit(solution)/shard_map/ppermute | solution.py:59
  72.5 9.8 %collective-permute-start.5 = (f32[8,4097]{1,0:T(8,128)S(1)}, f32[8,4097]{1,0:T(8,128)S(1)}, u32[]{:S(2)}, u32[]{:S(2)}) collective-permute-start(f32[8,4097]{1,0:T(8,128)S(1)} %add.344), channel_id=1, source_target_pairs={{0,32},{16,48},{32,0},{48,16},{64,96},{80,112},{96,64},{112,80},{1... | collective-permute-start | bytes 393320 | tf_op jit(solution)/shard_map/ppermute | solution.py:27
  82.3 10.9 %collective-permute-start.6 = (f32[8,4097]{1,0:T(8,128)S(1)}, f32[8,4097]{1,0:T(8,128)S(1)}, u32[]{:S(2)}, u32[]{:S(2)}) collective-permute-start(f32[8,4097]{1,0:T(8,128)S(1)} %add.345), channel_id=1, source_target_pairs={{0,64},{16,80},{32,96},{48,112},{64,0},{80,16},{96,32},{112,48},{1... | collective-permute-start | bytes 393320 | tf_op jit(solution)/shard_map/ppermute | solution.py:27
  82.9 20.0 %collective-permute-start.20 = (f32[8,192]{1,0:T(8,128)}, f32[8,192]{1,0:T(8,128)S(1)}, u32[]{:S(2)}, u32[]{:S(2)}) collective-permute-start(f32[8,192]{1,0:T(8,128)} %get-tuple-element.49), channel_id=1, source_target_pairs={{1,0},{2,1},{3,2},{4,3},{5,4},{6,5},{7,6},{8,7},{9,8},{10,9},{11,1... | collective-permute-start | bytes 18440 | tf_op jit(solution)/shard_map/ppermute | solution.py:59
  88.2 14.7 %collective-permute-start.21 = (f32[8,192]{1,0:T(8,128)}, f32[8,192]{1,0:T(8,128)}, u32[]{:S(2)}, u32[]{:S(2)}) collective-permute-start(f32[8,192]{1,0:T(8,128)} %get-tuple-element.48), channel_id=1, source_target_pairs={{16,1},{17,2},{18,3},{19,4},{20,5},{21,6},{22,7},{23,8},{24,9},{25... | collective-permute-start | bytes 18440 | tf_op jit(solution)/shard_map/ppermute | solution.py:59
  90.2 12.7 %collective-permute-start.22 = (f32[8,192]{1,0:T(8,128)S(1)}, f32[8,192]{1,0:T(8,128)}, u32[]{:S(2)}, u32[]{:S(2)}) collective-permute-start(f32[8,192]{1,0:T(8,128)S(1)} %get-tuple-element.47), channel_id=1, source_target_pairs={{16,0},{17,1},{18,2},{19,3},{20,4},{21,5},{22,6},{23,7},{24,8},{25... | collective-permute-start | bytes 18440 | tf_op jit(solution)/shard_map/ppermute | solution.py:59
  93.2 9.7 %collective-permute-start.23 = (f32[8,192]{1,0:T(8,128)S(1)}, f32[8,192]{1,0:T(8,128)}, u32[]{:S(2)}, u32[]{:S(2)}) collective-permute-start(f32[8,192]{1,0:T(8,128)S(1)} %get-tuple-element.46), channel_id=1, source_target_pairs={{17,0},{18,1},{19,2},{20,3},{21,4},{22,5},{23,6},{24,7},{25,8},{26... | collective-permute-start | bytes 18440 | tf_op jit(solution)/shard_map/ppermute | solution.py:59
  101.5 6.9 %collective-permute-start.7 = (f32[8,4097]{1,0:T(8,128)S(1)}, f32[8,4097]{1,0:T(8,128)S(1)}, u32[]{:S(2)}, u32[]{:S(2)}) collective-permute-start(f32[8,4097]{1,0:T(8,128)S(1)} %add.346), channel_id=1, source_target_pairs={{0,128},{16,144},{32,160},{48,176},{64,192},{80,208},{96,224},{112... | collective-permute-start | bytes 393320 | tf_op jit(solution)/shard_map/ppermute | solution.py:27
  121.2 25.6 %collective-permute-start.8 = (bf16[3,8,8,192]{3,2,1,0:T(8,128)(2,1)S(1)}, bf16[3,8,8,192]{3,2,1,0:T(8,128)(2,1)S(1)}, u32[]{:S(2)}, u32[]{:S(2)}) collective-permute-start(bf16[3,8,8,192]{3,2,1,0:T(8,128)(2,1)S(1)} %get-tuple-element.61), channel_id=1, source_target_pairs={{0,17},{1,18},{2,19},{3,20},{4,21},{5,22},{6,23},{7,24},{8,25},{9,... | collective-permute-start | bytes 221192 | tf_op jit(solution)/shard_map/ppermute | solution.py:59
  123.1 25.6 %collective-permute-start.9 = (bf16[3,8,8,192]{3,2,1,0:T(8,128)(2,1)S(1)}, bf16[3,8,8,192]{3,2,1,0:T(8,128)(2,1)S(1)}, u32[]{:S(2)}, u32[]{:S(2)}) collective-permute-start(bf16[3,8,8,192]{3,2,1,0:T(8,128)(2,1)S(1)} %get-tuple-element.67), channel_id=1, source_target_pairs={{0,16},{1,17},{2,18},{3,19},{4,20},{5,21},{6,22},{7,23},{8,24},{9,... | collective-permute-start | bytes 221192 | tf_op jit(solution)/shard_map/ppermute | solution.py:59
  128.6 25.1 %collective-permute-start.10 = (bf16[3,8,8,192]{3,2,1,0:T(8,128)(2,1)S(1)}, bf16[3,8,8,192]{3,2,1,0:T(8,128)(2,1)S(1)}, u32[]{:S(2)}, u32[]{:S(2)}) collective-permute-start(bf16[3,8,8,192]{3,2,1,0:T(8,128)(2,1)S(1)} %get-tuple-element.62), channel_id=1, source_target_pairs={{1,16},{2,17},{3,18},{4,19},{5,20},{6,21},{7,22},{8,23},{9,24},{10... | collective-permute-start | bytes 221192 | tf_op jit(solution)/shard_map/ppermute | solution.py:59
  134.1 26.9 %collective-permute-start.11 = (bf16[3,8,8,192]{3,2,1,0:T(8,128)(2,1)S(1)}, bf16[3,8,8,192]{3,2,1,0:T(8,128)(2,1)S(1)}, u32[]{:S(2)}, u32[]{:S(2)}) collective-permute-start(bf16[3,8,8,192]{3,2,1,0:T(8,128)(2,1)S(1)} %get-tuple-element.63), channel_id=1, source_target_pairs={{0,1},{1,2},{2,3},{3,4},{4,5},{5,6},{6,7},{7,8},{8,9},{9,10},{10,1... | collective-permute-start | bytes 221192 | tf_op jit(solution)/shard_map/ppermute | solution.py:59
  136.0 25.0 %collective-permute-start.12 = (bf16[3,8,8,192]{3,2,1,0:T(8,128)(2,1)S(1)}, bf16[3,8,8,192]{3,2,1,0:T(8,128)(2,1)S(1)}, u32[]{:S(2)}, u32[]{:S(2)}) collective-permute-start(bf16[3,8,8,192]{3,2,1,0:T(8,128)(2,1)S(1)} %get-tuple-element.64), channel_id=1, source_target_pairs={{1,0},{2,1},{3,2},{4,3},{5,4},{6,5},{7,6},{8,7},{9,8},{10,9},{11,1... | collective-permute-start | bytes 221192 | tf_op jit(solution)/shard_map/ppermute | solution.py:59
  146.8 14.3 %collective-permute-start.13 = (bf16[3,8,8,192]{3,2,1,0:T(8,128)(2,1)S(1)}, bf16[3,8,8,192]{3,2,1,0:T(8,128)(2,1)S(1)}, u32[]{:S(2)}, u32[]{:S(2)}) collective-permute-start(bf16[3,8,8,192]{3,2,1,0:T(8,128)(2,1)S(1)} %get-tuple-element.65), channel_id=1, source_target_pairs={{16,1},{17,2},{18,3},{19,4},{20,5},{21,6},{22,7},{23,8},{24,9},{25... | collective-permute-start | bytes 221192 | tf_op jit(solution)/shard_map/ppermute | solution.py:59
  148.7 12.4 %collective-permute-start.14 = (bf16[3,8,8,192]{3,2,1,0:T(8,128)(2,1)S(1)}, bf16[3,8,8,192]{3,2,1,0:T(8,128)(2,1)S(1)}, u32[]{:S(2)}, u32[]{:S(2)}) collective-permute-start(bf16[3,8,8,192]{3,2,1,0:T(8,128)(2,1)S(1)} %get-tuple-element.66), channel_id=1, source_target_pairs={{16,0},{17,1},{18,2},{19,3},{20,4},{21,5},{22,6},{23,7},{24,8},{25... | collective-permute-start | bytes 221192 | tf_op jit(solution)/shard_map/ppermute | solution.py:59
  153.7 9.5 %collective-permute-start.15 = (bf16[3,8,8,192]{3,2,1,0:T(8,128)(2,1)S(1)}, bf16[3,8,8,192]{3,2,1,0:T(8,128)(2,1)S(1)}, u32[]{:S(2)}, u32[]{:S(2)}) collective-permute-start(bf16[3,8,8,192]{3,2,1,0:T(8,128)(2,1)S(1)} %get-tuple-element.68), channel_id=1, source_target_pairs={{17,0},{18,1},{19,2},{20,3},{21,4},{22,5},{23,6},{24,7},{25,8},{26... | collective-permute-start | bytes 221192 | tf_op jit(solution)/shard_map/ppermute | solution.py:59
  174.7 7.5 %collective-permute-start.25 = (f32[8]{0:T(128)S(1)}, f32[8]{0:T(128)S(1)}, u32[]{:S(2)}, u32[]{:S(2)}) collective-permute-start(f32[8]{0:T(128)S(1)} %add.388), channel_id=1, source_target_pairs={{0,2},{1,3},{2,0},{3,1},{4,6},{5,7},{6,4},{7,5},{8,10},{9,11},{10,... | collective-permute-start | bytes 104 | tf_op jit(solution)/shard_map/ppermute | solution.py:27
  182.2 4.9 %collective-permute-start.26 = (f32[8]{0:T(128)S(1)}, f32[8]{0:T(128)S(1)}, u32[]{:S(2)}, u32[]{:S(2)}) collective-permute-start(f32[8]{0:T(128)S(1)} %add.389), channel_id=1, source_target_pairs={{0,4},{1,5},{2,6},{3,7},{4,0},{5,1},{6,2},{7,3},{8,12},{9,13},{10,... | collective-permute-start | bytes 104 | tf_op jit(solution)/shard_map/ppermute | solution.py:27
  187.1 5.1 %collective-permute-start.27 = (f32[8]{0:T(128)S(1)}, f32[8]{0:T(128)S(1)}, u32[]{:S(2)}, u32[]{:S(2)}) collective-permute-start(f32[8]{0:T(128)S(1)} %add.390), channel_id=1, source_target_pairs={{0,8},{1,9},{2,10},{3,11},{4,12},{5,13},{6,14},{7,15},{8,0},{9,1},... | collective-permute-start | bytes 104 | tf_op jit(solution)/shard_map/ppermute | solution.py:27
  203.9 5.1 %collective-permute-start.31 = (f32[8]{0:T(128)S(1)}, f32[8]{0:T(128)S(1)}, u32[]{:S(2)}, u32[]{:S(2)}) collective-permute-start(f32[8]{0:T(128)S(1)} %add.394), channel_id=1, source_target_pairs={{0,128},{16,144},{32,160},{48,176},{64,192},{80,208},{96,224},{112... | collective-permute-start | bytes 104 | tf_op jit(solution)/shard_map/ppermute | solution.py:27
  211.3 11.2 %collective-permute-start.32 = (f32[8,4097]{1,0:T(8,128)S(1)}, f32[8,4097]{1,0:T(8,128)S(1)}, u32[]{:S(2)}, u32[]{:S(2)}) collective-permute-start(f32[8,4097]{1,0:T(8,128)S(1)} %pad_maximum_fusion.17), channel_id=1, source_target_pairs={{0,1},{1,0},{2,3},{3,2},{4,5},{5,4},{6,7},{7,6},{8,9},{9,8},{10,11... | collective-permute-start | bytes 393320 | tf_op jit(solution)/shard_map/ppermute | solution.py:27
  222.5 12.3 %collective-permute-start.33 = (f32[8,4097]{1,0:T(8,128)S(1)}, f32[8,4097]{1,0:T(8,128)S(1)}, u32[]{:S(2)}, u32[]{:S(2)}) collective-permute-start(f32[8,4097]{1,0:T(8,128)S(1)} %fusion.101), channel_id=1, source_target_pairs={{0,2},{1,3},{2,0},{3,1},{4,6},{5,7},{6,4},{7,5},{8,10},{9,11},{10,... | collective-permute-start | bytes 393320 | tf_op jit(solution)/shard_map/ppermute | solution.py:27
  234.8 5.7 %collective-permute-start.34 = (f32[8,4097]{1,0:T(8,128)S(1)}, f32[8,4097]{1,0:T(8,128)S(1)}, u32[]{:S(2)}, u32[]{:S(2)}) collective-permute-start(f32[8,4097]{1,0:T(8,128)S(1)} %add.397), channel_id=1, source_target_pairs={{0,4},{1,5},{2,6},{3,7},{4,0},{5,1},{6,2},{7,3},{8,12},{9,13},{10,... | collective-permute-start | bytes 393320 | tf_op jit(solution)/shard_map/ppermute | solution.py:27
  240.5 6.6 %collective-permute-start.35 = (f32[8,4097]{1,0:T(8,128)S(1)}, f32[8,4097]{1,0:T(8,128)S(1)}, u32[]{:S(2)}, u32[]{:S(2)}) collective-permute-start(f32[8,4097]{1,0:T(8,128)S(1)} %add.398), channel_id=1, source_target_pairs={{0,8},{1,9},{2,10},{3,11},{4,12},{5,13},{6,14},{7,15},{8,0},{9,1},... | collective-permute-start | bytes 393320 | tf_op jit(solution)/shard_map/ppermute | solution.py:27
  247.1 5.3 %collective-permute-start.36 = (f32[8,4097]{1,0:T(8,128)S(1)}, f32[8,4097]{1,0:T(8,128)S(1)}, u32[]{:S(2)}, u32[]{:S(2)}) collective-permute-start(f32[8,4097]{1,0:T(8,128)S(1)} %add.399), channel_id=1, source_target_pairs={{0,16},{16,0},{32,48},{48,32},{64,80},{80,64},{96,112},{112,96},{1... | collective-permute-start | bytes 393320 | tf_op jit(solution)/shard_map/ppermute | solution.py:27
  252.4 6.0 %collective-permute-start.37 = (f32[8,4097]{1,0:T(8,128)S(1)}, f32[8,4097]{1,0:T(8,128)S(1)}, u32[]{:S(2)}, u32[]{:S(2)}) collective-permute-start(f32[8,4097]{1,0:T(8,128)S(1)} %add.400), channel_id=1, source_target_pairs={{0,32},{16,48},{32,0},{48,16},{64,96},{80,112},{96,64},{112,80},{1... | collective-permute-start | bytes 393320 | tf_op jit(solution)/shard_map/ppermute | solution.py:27
  258.4 5.9 %collective-permute-start.38 = (f32[8,4097]{1,0:T(8,128)S(1)}, f32[8,4097]{1,0:T(8,128)S(1)}, u32[]{:S(2)}, u32[]{:S(2)}) collective-permute-start(f32[8,4097]{1,0:T(8,128)S(1)} %add.401), channel_id=1, source_target_pairs={{0,64},{16,80},{32,96},{48,112},{64,0},{80,16},{96,32},{112,48},{1... | collective-permute-start | bytes 393320 | tf_op jit(solution)/shard_map/ppermute | solution.py:27
  264.4 6.6 %collective-permute-start.39 = (f32[8,4097]{1,0:T(8,128)S(1)}, f32[8,4097]{1,0:T(8,128)S(1)}, u32[]{:S(2)}, u32[]{:S(2)}) collective-permute-start(f32[8,4097]{1,0:T(8,128)S(1)} %add.402), channel_id=1, source_target_pairs={{0,128},{16,144},{32,160},{48,176},{64,192},{80,208},{96,224},{112... | collective-permute-start | bytes 393320 | tf_op jit(solution)/shard_map/ppermute | solution.py:27
  279.7 23.4 %collective-permute-start.40 = (bf16[3,8,8,192]{3,2,1,0:T(8,128)(2,1)S(1)}, bf16[3,8,8,192]{3,2,1,0:T(8,128)(2,1)S(1)}, u32[]{:S(2)}, u32[]{:S(2)}) collective-permute-start(bf16[3,8,8,192]{3,2,1,0:T(8,128)(2,1)S(1)} %get-tuple-element.53), channel_id=1, source_target_pairs={{0,17},{1,18},{2,19},{3,20},{4,21},{5,22},{6,23},{7,24},{8,25},{9,... | collective-permute-start | bytes 221192 | tf_op jit(solution)/shard_map/ppermute | solution.py:59
  281.6 23.4 %collective-permute-start.41 = (bf16[3,8,8,192]{3,2,1,0:T(8,128)(2,1)S(1)}, bf16[3,8,8,192]{3,2,1,0:T(8,128)(2,1)S(1)}, u32[]{:S(2)}, u32[]{:S(2)}) collective-permute-start(bf16[3,8,8,192]{3,2,1,0:T(8,128)(2,1)S(1)} %get-tuple-element.59), channel_id=1, source_target_pairs={{0,16},{1,17},{2,18},{3,19},{4,20},{5,21},{6,22},{7,23},{8,24},{9,... | collective-permute-start | bytes 221192 | tf_op jit(solution)/shard_map/ppermute | solution.py:59
  285.5 22.9 %collective-permute-start.42 = (bf16[3,8,8,192]{3,2,1,0:T(8,128)(2,1)S(1)}, bf16[3,8,8,192]{3,2,1,0:T(8,128)(2,1)S(1)}, u32[]{:S(2)}, u32[]{:S(2)}) collective-permute-start(bf16[3,8,8,192]{3,2,1,0:T(8,128)(2,1)S(1)} %get-tuple-element.54), channel_id=1, source_target_pairs={{1,16},{2,17},{3,18},{4,19},{5,20},{6,21},{7,22},{8,23},{9,24},{10... | collective-permute-start | bytes 221192 | tf_op jit(solution)/shard_map/ppermute | solution.py:59
  292.7 22.9 %collective-permute-start.43 = (bf16[3,8,8,192]{3,2,1,0:T(8,128)(2,1)S(1)}, bf16[3,8,8,192]{3,2,1,0:T(8,128)(2,1)S(1)}, u32[]{:S(2)}, u32[]{:S(2)}) collective-permute-start(bf16[3,8,8,192]{3,2,1,0:T(8,128)(2,1)S(1)} %get-tuple-element.55), channel_id=1, source_target_pairs={{0,1},{1,2},{2,3},{3,4},{4,5},{5,6},{6,7},{7,8},{8,9},{9,10},{10,1... | collective-permute-start | bytes 221192 | tf_op jit(solution)/shard_map/ppermute | solution.py:59
  294.6 21.0 %collective-permute-start.44 = (bf16[3,8,8,192]{3,2,1,0:T(8,128)(2,1)S(1)}, bf16[3,8,8,192]{3,2,1,0:T(8,128)(2,1)S(1)}, u32[]{:S(2)}, u32[]{:S(2)}) collective-permute-start(bf16[3,8,8,192]{3,2,1,0:T(8,128)(2,1)S(1)} %get-tuple-element.56), channel_id=1, source_target_pairs={{1,0},{2,1},{3,2},{4,3},{5,4},{6,5},{7,6},{8,7},{9,8},{10,9},{11,1... | collective-permute-start | bytes 221192 | tf_op jit(solution)/shard_map/ppermute | solution.py:59
  303.1 12.5 %collective-permute-start.45 = (bf16[3,8,8,192]{3,2,1,0:T(8,128)(2,1)S(1)}, bf16[3,8,8,192]{3,2,1,0:T(8,128)(2,1)S(1)}, u32[]{:S(2)}, u32[]{:S(2)}) collective-permute-start(bf16[3,8,8,192]{3,2,1,0:T(8,128)(2,1)S(1)} %get-tuple-element.57), channel_id=1, source_target_pairs={{16,1},{17,2},{18,3},{19,4},{20,5},{21,6},{22,7},{23,8},{24,9},{25... | collective-permute-start | bytes 221192 | tf_op jit(solution)/shard_map/ppermute | solution.py:59
  305.0 10.6 %collective-permute-start.46 = (bf16[3,8,8,192]{3,2,1,0:T(8,128)(2,1)S(1)}, bf16[3,8,8,192]{3,2,1,0:T(8,128)(2,1)S(1)}, u32[]{:S(2)}, u32[]{:S(2)}) collective-permute-start(bf16[3,8,8,192]{3,2,1,0:T(8,128)(2,1)S(1)} %get-tuple-element.58), channel_id=1, source_target_pairs={{16,0},{17,1},{18,2},{19,3},{20,4},{21,5},{22,6},{23,7},{24,8},{25... | collective-permute-start | bytes 221192 | tf_op jit(solution)/shard_map/ppermute | solution.py:59
  308.4 9.3 %collective-permute-start.47 = (bf16[3,8,8,192]{3,2,1,0:T(8,128)(2,1)S(1)}, bf16[3,8,8,192]{3,2,1,0:T(8,128)(2,1)S(1)}, u32[]{:S(2)}, u32[]{:S(2)}) collective-permute-start(bf16[3,8,8,192]{3,2,1,0:T(8,128)(2,1)S(1)} %get-tuple-element.60), channel_id=1, source_target_pairs={{17,0},{18,1},{19,2},{20,3},{21,4},{22,5},{23,6},{24,7},{25,8},{26... | collective-permute-start | bytes 221192 | tf_op jit(solution)/shard_map/ppermute | solution.py:59
  325.2 5.9 %collective-permute-start.48 = (f32[8]{0:T(128)S(1)}, f32[8]{0:T(128)S(1)}, u32[]{:S(2)}, u32[]{:S(2)}) collective-permute-start(f32[8]{0:T(128)S(1)} %get-tuple-element.82), channel_id=1, source_target_pairs={{0,1},{1,0},{2,3},{3,2},{4,5},{5,4},{6,7},{7,6},{8,9},{9,8},{10,11... | collective-permute-start | bytes 104 | tf_op jit(solution)/shard_map/ppermute | solution.py:27
  331.1 7.5 %collective-permute-start.49 = (f32[8]{0:T(128)S(1)}, f32[8]{0:T(128)S(1)}, u32[]{:S(2)}, u32[]{:S(2)}) collective-permute-start(f32[8]{0:T(128)S(1)} %add.435), channel_id=1, source_target_pairs={{0,2},{1,3},{2,0},{3,1},{4,6},{5,7},{6,4},{7,5},{8,10},{9,11},{10,... | collective-permute-start | bytes 104 | tf_op jit(solution)/shard_map/ppermute | solution.py:27
  342.1 5.1 %collective-permute-start.51 = (f32[8]{0:T(128)S(1)}, f32[8]{0:T(128)S(1)}, u32[]{:S(2)}, u32[]{:S(2)}) collective-permute-start(f32[8]{0:T(128)S(1)} %add.437), channel_id=1, source_target_pairs={{0,8},{1,9},{2,10},{3,11},{4,12},{5,13},{6,14},{7,15},{8,0},{9,1},... | collective-permute-start | bytes 104 | tf_op jit(solution)/shard_map/ppermute | solution.py:27
  358.8 5.1 %collective-permute-start.55 = (f32[8]{0:T(128)S(1)}, f32[8]{0:T(128)S(1)}, u32[]{:S(2)}, u32[]{:S(2)}) collective-permute-start(f32[8]{0:T(128)S(1)} %add.441), channel_id=1, source_target_pairs={{0,128},{16,144},{32,160},{48,176},{64,192},{80,208},{96,224},{112... | collective-permute-start | bytes 104 | tf_op jit(solution)/shard_map/ppermute | solution.py:27
  (28 other events, 525.6 us)
